TPU v7x, 128 devices: a whole 4x4x4 slice. The times are simulated.
128 devices in a mesh: ctx: 32 (over y, z, core), tp: 4 (over x).
Axes of the slice: x: 4, y: 4, z: 4, core: 2. Of those that a mesh axis runs over, the one named last changes fastest.
Arguments:
- hidden_in: bfloat16 [16384, 4608], P('ctx'), may hold values from -5.4 to 5.4
- pre_gain: float32 [4608], replicated, may hold values from 0.25 to 1.75
- w_query: bfloat16 [4608, 2048], P(None, 'tp'), may hold values from -0.677644 to 0.677644
- w_key: bfloat16 [4608, 1024], P(None, 'tp'), may hold values from -0.058925565 to 0.058925565
- w_value: bfloat16 [4608, 1024], P(None, 'tp'), may hold values from -0.09375 to 0.09375
- w_out: bfloat16 [2048, 4608], P('tp'), may hold values from -0.26516504 to 0.26516504
- post_gain: float32 [4608], P('tp'), may hold values from 0.25 to 1.75
Outputs:
- layer_out: bfloat16 [16384, 4608], P('ctx', 'tp')
- sink_share: float32 [16384], P('ctx')
All inputs are finite; a program needn't handle non-finite values.
Results may differ from a plain program's by a relative error of at most 0.0095.
The roundings to bfloat16 on the way count: a program that leaves them out, or rounds other values in their place, can miss the bound.
Values may be sent and summed in bfloat16 or wider, within the bound.
No kernel may reach another device: no remote copies, remote signals or barrier semaphores. Data moves between devices by JAX's collectives and lax.ppermute only.
A program may use at most 192 MiB of HBM per device.

v0:
```python
import jax
import jax.numpy as jnp
from jax import lax
from jax.sharding import PartitionSpec as P

D = 4608
QHEADS = 16
HEAD = 128
WINDOW = 4096
SINKS = 4


def shifted(x, axis, by):
    devices = lax.axis_size(axis)
    pairs = [(i, i + by) for i in range(devices) if 0 <= i + by < devices]
    return lax.ppermute(x, axis, pairs)


def spread(value, axis, source):
    kept = jnp.where(lax.axis_index(axis) == source, value, 0).astype(value.dtype)
    return lax.psum(kept, axis)


def rope_tables(positions):
    index = jnp.arange(0, HEAD, 2).astype(jnp.float32)
    inverse = jnp.exp(-jnp.log(jnp.float32(10000.0)) * index / HEAD)
    angles = positions.astype(jnp.float32)[:, None] * inverse[None, :]
    angles = jnp.concatenate([angles, angles], axis=1)
    return (jnp.cos(angles)[:, None, :], jnp.sin(angles)[:, None, :])


def rotate(values, cosine_table, sine_table):
    half = values.shape[-1] // 2
    turned = jnp.concatenate([-values[..., half:], values[..., :half]], axis=-1)
    return values * cosine_table + turned * sine_table


def project_keys(states, w_key, w_value, positions):
    count = states.shape[0]
    cosine_table, sine_table = rope_tables(positions)
    keys = jnp.dot(states, w_key, preferred_element_type=jnp.float32).reshape(count, -1, HEAD)
    keys = rotate(keys, cosine_table, sine_table).astype(jnp.bfloat16).reshape(count, -1)
    values = jnp.dot(states, w_value, preferred_element_type=jnp.float32).astype(jnp.bfloat16)
    return (keys, values)


def on_device(hidden_in, pre_gain, w_query, w_key, w_value, w_out, post_gain):
    tok_rows = hidden_in.shape[0]
    local_q = w_query.shape[1] // HEAD
    local_kv = w_key.shape[1] // HEAD
    group = local_q // local_kv
    offset = lax.axis_index("ctx") * tok_rows
    inputs = hidden_in.astype(jnp.float32)
    normed = (
        inputs * lax.rsqrt(jnp.mean(inputs * inputs, axis=-1, keepdims=True) + 1e-06) * pre_gain
    ).astype(jnp.bfloat16)
    positions = offset + jnp.arange(tok_rows, dtype=jnp.int32)
    cosine_table, sine_table = rope_tables(positions)
    query = jnp.dot(normed, w_query, preferred_element_type=jnp.float32).reshape(
        tok_rows, local_q, HEAD
    )
    query = (
        rotate(query, cosine_table, sine_table)
        .astype(jnp.bfloat16)
        .reshape(tok_rows, local_kv, group, HEAD)
    )
    keys, values = project_keys(normed, w_key, w_value, positions)
    reach = WINDOW // tok_rows
    pieces = []
    for distance in range(reach, 0, -1):
        pieces.append(shifted((keys, values), "ctx", distance))
    keys_all = jnp.concatenate([piece[0] for piece in pieces] + [keys], axis=0)
    values_all = jnp.concatenate([piece[1] for piece in pieces] + [values], axis=0)
    sink_keys, sink_values = (spread(keys[:SINKS], "ctx", 0), spread(values[:SINKS], "ctx", 0))
    sink_keys = sink_keys.reshape(SINKS, local_kv, HEAD)
    sink_values = sink_values.reshape(SINKS, local_kv, HEAD)
    block_rows = min(512, tok_rows)
    span = WINDOW + block_rows

    def one_block(block_index):
        start = block_index * block_rows
        key_block = keys_all.reshape(span, local_kv, HEAD)
        value_block = values_all.reshape(span, local_kv, HEAD)
        scores = (
            jnp.einsum("qkgd,lkd->kgql", query, key_block, preferred_element_type=jnp.float32)
            / 12.0
        )
        scores = 50.0 * jnp.tanh(scores / 50.0)
        sink_scores = (
            jnp.einsum("qkgd,lkd->kgql", query, sink_keys, preferred_element_type=jnp.float32)
            / 12.0
        )
        sink_scores = 50.0 * jnp.tanh(sink_scores / 50.0)
        query_pos = offset + start + jnp.arange(block_rows, dtype=jnp.int32)
        key_pos = offset + start - WINDOW + jnp.arange(span, dtype=jnp.int32)
        distance_map = query_pos[:, None] - key_pos[None, :]
        live = (key_pos[None, :] >= SINKS) & (distance_map >= 0) & (distance_map < WINDOW)
        sink_live = query_pos[:, None] - jnp.arange(SINKS, dtype=jnp.int32)[None, :] >= 0
        expo = jnp.where(live, jnp.exp(scores), 0.0)
        sink_expo = jnp.where(sink_live, jnp.exp(sink_scores), 0.0)
        total = jnp.sum(expo, axis=-1) + jnp.sum(sink_expo, axis=-1)
        weight = expo / total[..., None]
        sink_weight = sink_expo / total[..., None]
        sink_sum = jnp.sum(sink_expo, axis=-1)
        attended = jnp.einsum(
            "kgql,lkd->qkgd",
            weight.astype(jnp.bfloat16),
            value_block,
            preferred_element_type=jnp.float32,
        )
        attended = attended + jnp.einsum(
            "kgql,lkd->qkgd",
            sink_weight.astype(jnp.bfloat16),
            sink_values,
            preferred_element_type=jnp.float32,
        )
        attended = attended.astype(jnp.bfloat16).reshape(block_rows, local_q * HEAD)
        return (attended, jnp.sum(sink_sum, axis=(0, 1)))

    attended, sink_sums = lax.map(one_block, jnp.arange(tok_rows // block_rows, dtype=jnp.int32))
    attended = attended.reshape(tok_rows, local_q * HEAD)
    sink_sums = sink_sums.reshape(tok_rows)
    cols_dev = post_gain.shape[0]
    partial_rows = jnp.dot(attended, w_out, preferred_element_type=jnp.float32)
    projected = lax.psum_scatter(partial_rows, "tp", scatter_dimension=1, tiled=True)
    squares = jnp.sum(projected * projected, axis=-1)
    total_squares, total_sinks = lax.psum((squares, sink_sums), "tp")
    post = projected * lax.rsqrt(total_squares / D + 1e-06)[:, None] * post_gain
    own_cols = lax.dynamic_slice_in_dim(inputs, lax.axis_index("tp") * cols_dev, cols_dev, 1)
    layer_out = (own_cols + post).astype(jnp.bfloat16)
    sink_share = jnp.log(total_sinks / QHEADS)
    return (layer_out, sink_share)


def solution(mesh):
    return jax.shard_map(
        on_device,
        mesh=mesh,
        in_specs=(
            P("ctx", None),
            P(),
            P(None, "tp"),
            P(None, "tp"),
            P(None, "tp"),
            P("tp", None),
            P("tp"),
        ),
        out_specs=(P("ctx", "tp"), P("ctx")),
        check_vma=False,
    )
```

profile of v0, /device:TPU:8, one launch (start us, length us, event | category | flops | bytes accessed | tf_op | source)
XLA Modules:
  0.0 350.7 jit_solution(993814466093420945)
XLA Ops:
  8.6 3.6 %multiply_reduce_fusion = f32[512]{0:T(512)S(1)} fusion(bf16[512,4608]{1,0:T(8,128)(2,1)} %param.7), kind=kLoop, calls=%fused_computation.7 | loop fusion | flops 7077376 | bytes 4720640 | tf_op jit(solution)/shard_map/reduce_sum | solution.py:55
  16.2 3.6 %collective-permute-start.8 = (bf16[512,256]{0,1:T(8,128)(2,1)}, bf16[512,256]{0,1:T(8,128)(2,1)}, u32[]{:S(2)}, u32[]{:S(2)}) collective-permute-start(bf16[512,256]{0,1:T(8,128)(2,1)} %fusion.15), channel_id=1, source_target_pairs={{0,32},{4,36},{8,40},{12,44},{16,48},{20,52},{24,56},{28,60},{32,6... | collective-permute-start | bytes 786440 | tf_op jit(solution)/shard_map/ppermute | solution.py:16
  19.9 5.1 %collective-permute-start.9 = (bf16[512,256]{0,1:T(8,128)(2,1)}, bf16[512,256]{0,1:T(8,128)(2,1)}, u32[]{:S(2)}, u32[]{:S(2)}) collective-permute-start(bf16[512,256]{0,1:T(8,128)(2,1)} %fusion.15), channel_id=1, source_target_pairs={{0,28},{4,32},{8,36},{12,40},{16,44},{20,48},{24,52},{28,56},{32,6... | collective-permute-start | bytes 786440 | tf_op jit(solution)/shard_map/ppermute | solution.py:16
  25.0 3.0 collective-permute-start.10
  28.0 2.5 collective-permute-start.11
  30.5 5.2 %convolution_convert_fusion = bf16[512,256]{1,0:T(8,128)(2,1)} fusion(bf16[4608,256]{1,0:T(8,128)(2,1)} %param.11, f32[4608]{0:T(1024)S(1)} %copy-done.14, f32[512]{0:T(512)S(1)} %add_rsqrt_fusion.1, bf16[512,4608]{1,0:T(8,128)(2,1)} %param.7), kind=kOutput, calls=%fused_computation.16 | convolution fusion | flops 1217527808 | bytes 7360512 | tf_op jit(solution)/shard_map/dot_general | solution.py:43
  38.8 6.9 %fusion.29 = f32[512,512]{0,1:T(8,128)S(1)} fusion(bf16[4608,512]{1,0:T(8,128)(2,1)} %param.9, f32[4608]{0:T(1024)S(1)} %copy-done.15, f32[512]{0:T(512)} %copy-done.13, bf16[512,4608]{1,0:T(8,128)(2,1)} %param.7), kind=kOutput, calls=%fused_computation.75 | convolution fusion | flops 2425356288 | bytes 10506240 | tf_op jit(solution)/shard_map/dot_general | solution.py:59
  51.4 4.7 %fusion.3 = pred[512,4608]{0,1:T(8,128)(4,1)} fusion(s32[4608]{0:T(1024)S(1)} %copy-done.11, s32[512]{0:T(512)S(1)} %iota_add_fusion.1, pred[4608]{0:T(1024)(128)(4,1)S(1)} %broadcast_compare_fusion), kind=kLoop, calls=%fused_computation.9 | loop fusion | flops 11796480 | bytes 2384384 | tf_op jit(solution)/shard_map/while/body/eval_jaxpr/and | solution.py:97
  57.5 54.7 %all-reduce.1 = (bf16[4,2,128]{2,0,1:T(4,128)(2,1)S(1)}, bf16[4,2,128]{2,0,1:T(4,128)(2,1)S(1)}) all-reduce(bf16[4,2,128]{2,0,1:T(4,128)(2,1)S(1)} %fusion.21, bf16[4,2,128]{2,0,1:T(4,128)(2,1)S(1)} %fusion.22), channel_id=1, replica_groups=mesh['ctx'=32,'tp'=4] {'ctx'}, use_global_device_ids=true, to_apply=%region_2.3 | all-reduce | flops 2048 | bytes 8192 | tf_op jit(solution)/shard_map/psum | solution.py:21
  120.5 9.5 %collective-permute-start.2 = (bf16[512,256]{1,0:T(8,128)(2,1)}, bf16[512,256]{1,0:T(8,128)(2,1)S(1)}, u32[]{:S(2)}, u32[]{:S(2)}) collective-permute-start(bf16[512,256]{1,0:T(8,128)(2,1)} %convolution_convert_fusion), channel_id=1, source_target_pairs={{0,24},{4,28},{8,32},{12,36},{16,40},{20,44},{24,48},{28,52},{32,5... | collective-permute-start | bytes 786440 | tf_op jit(solution)/shard_map/ppermute | solution.py:16
  130.7 5.4 %collective-permute-start.3 = (bf16[512,256]{1,0:T(8,128)(2,1)}, bf16[512,256]{1,0:T(8,128)(2,1)S(1)}, u32[]{:S(2)}, u32[]{:S(2)}) collective-permute-start(bf16[512,256]{1,0:T(8,128)(2,1)} %convolution_convert_fusion), channel_id=1, source_target_pairs={{0,20},{4,24},{8,28},{12,32},{16,36},{20,40},{24,44},{28,48},{32,5... | collective-permute-start | bytes 786440 | tf_op jit(solution)/shard_map/ppermute | solution.py:16
  137.1 6.3 %collective-permute-start.4 = (bf16[512,256]{1,0:T(8,128)(2,1)}, bf16[512,256]{1,0:T(8,128)(2,1)S(1)}, u32[]{:S(2)}, u32[]{:S(2)}) collective-permute-start(bf16[512,256]{1,0:T(8,128)(2,1)} %convolution_convert_fusion), channel_id=1, source_target_pairs={{0,16},{4,20},{8,24},{12,28},{16,32},{20,36},{24,40},{28,44},{32,4... | collective-permute-start | bytes 786440 | tf_op jit(solution)/shard_map/ppermute | solution.py:16
  149.6 2.8 collective-permute-start.6
  162.8 3.7 %collective-permute-done.15 = bf16[512,256]{0,1:T(8,128)(2,1)} collective-permute-done((bf16[512,256]{0,1:T(8,128)(2,1)}, bf16[512,256]{0,1:T(8,128)(2,1)}, u32[]{:S(2)}, u32[]{:S(2)}) %collective-permute-start.15) | collective-permute-done | bytes 262176 | tf_op jit(solution)/shard_map/ppermute | solution.py:16
  169.2 3.2 collective-permute-done.6
  173.4 4.4 %collective-permute-done.7 = bf16[512,256]{1,0:T(8,128)(2,1)} collective-permute-done((bf16[512,256]{1,0:T(8,128)(2,1)}, bf16[512,256]{1,0:T(8,128)(2,1)}, u32[]{:S(2)}, u32[]{:S(2)}) %collective-permute-start.7) | collective-permute-done | bytes 262176 | tf_op jit(solution)/shard_map/ppermute | solution.py:16
  179.8 2.5 copy.34
  192.1 17.2 %fusion = (f32[2,2,512]{2,1,0:T(2,128)S(1)}, f32[2,4608,512,2]{2,1,3,0:T(8,128)}) fusion(pred[512,4608]{0,1:T(8,128)(4,1)S(1)} %copy-done.6, bf16[512,2,2,128]{3,0,2,1:T(8,128)(2,1)S(1)} %copy-done.9, bf16[4608,2,128]{2,0,1:T(8,128)(2,1)} %constant_dynamic-update-slice_fusion.9), kind=kOutput, calls=%fused_computation.2 | convolution fusion | flops 2453665792 | bytes 42999808 | tf_op jit(solution)/shard_map/while/body/eval_jaxpr/qkgd,lkd->kgql/dot_general | solution.py:85
  209.6 19.5 %fusion.7 = bf16[2,128,2,512]{3,1,2,0:T(8,128)(2,1)} fusion(f32[2,128,2,512]{3,1,2,0:T(8,128)S(1)} %fusion.18, bf16[4608,2,128,1]{0,2,3,1:T(8,128)(2,1)} %bitcast.80, f32[2,4608,512,2]{2,1,3,0:T(8,128)} %get-tuple-element.42, f32[2,2,512]{2,1,0:T(2,128)S(1)} %add.103, pred[512,4608]{0,1:T(8,128)(4,1)S(1)} %copy-done.6), kind=kOutput, calls=%fused_computation.15 | convolution fusion | flops 2463629312 | bytes 44048384 | tf_op jit(solution)/shard_map/while/body/eval_jaxpr/kgql,lkd->qkgd/dot_general | solution.py:105
  229.1 8.8 %fusion.33 = f32[512,4608]{1,0:T(8,128)} fusion(bf16[512,512]{0,1:T(8,128)(2,1)} %bitcast.81, bf16[512,4608]{1,0:T(8,128)(2,1)} %param.12), kind=kOutput, calls=%fused_computation.79 | convolution fusion | flops 2415919104 | bytes 14680064 | tf_op jit(solution)/shard_map/dot_general | solution.py:124
  237.9 7.2 %convert_element_type.56 = f32[512,4608]{1,0:T(8,128)} convert(bf16[512,4608]{1,0:T(8,128)(2,1)} %param.7) | non-fusion elementwise | flops 2359296 | bytes 14155776 | tf_op jit(solution)/shard_map/convert_element_type | solution.py:53
  245.1 83.7 %reduce-scatter.2.cloned.1.call-done = f32[512,1152]{1,0:T(8,128)} async-done(((f32[512,4608]{1,0:T(8,128)}), f32[512,1152]{1,0:T(8,128)}) %reduce-scatter.2.cloned.1.call-update) | async-done | bytes 2359312 | tf_op jit(solution)/shard_map/reduce_scatter | solution.py:125
  330.8 8.6 %all-reduce = (f32[512]{0:T(512)S(1)}, f32[512]{0:T(512)S(1)}) all-reduce(f32[512]{0:T(512)S(1)} %multiply_reduce_fusion.1, f32[512]{0:T(512)S(1)} %get-tuple-element.20), channel_id=1, replica_groups=mesh['ctx'=32,'tp'=4] {'tp'}, use_global_device_ids=true, to_apply=%region_7.8 | all-reduce | flops 1024 | bytes 8192 | tf_op jit(solution)/shard_map/psum | solution.py:127
  339.9 3.9 %add_convert_fusion = bf16[512,1152]{1,0:T(8,128)(2,1)} fusion(f32[512,1152]{1,0:T(8,128)} %reduce-scatter.2.cloned.1.call-done, f32[512,4608]{1,0:T(8,128)} %convert_element_type.56, s32[]{:T(128)S(6)} %select_n.30, f32[1152]{0:T(1024)S(1)} %copy-done.12, f32[512]{0:T(512)S(1)} %get-tuple-element.45), kind=kLoop, calls=%fused_computation.12 | loop fusion | flops 2359296 | bytes 5904900 | tf_op jit(solution)/shard_map/convert_element_type | solution.py:130
  (115 shorter events, 60.1 us)
Async XLA Ops:
  7.2 321.7 %reduce-scatter.2.cloned.1.call-start = ((), (), s32[]{:S(2)}) async-start(), calls=%async_computation.1 | async-start | bytes 11796480 | tf_op jit(solution)/shard_map/reduce_scatter | solution.py:125
  8.5 30.2 %copy-start.3 = (f32[512,128]{1,0:T(8,128)}, f32[512,128]{1,0:T(8,128)S(1)}, u32[]{:S(2)}) copy-start(f32[512,128]{1,0:T(8,128)S(1)} %get-tuple-element.39) | copy-start | bytes 786436
  12.6 17.9 %copy-start.13 = (f32[512]{0:T(512)}, f32[512]{0:T(512)S(1)}, u32[]{:S(2)}) copy-start(f32[512]{0:T(512)S(1)} %add_rsqrt_fusion.1) | copy-start | bytes 6148
  15.1 20.7 %copy-start.7 = (f32[512,2,128]{2,0,1:T(8,128)}, f32[512,2,128]{2,0,1:T(8,128)S(1)}, u32[]{:S(2)}) copy-start(f32[512,2,128]{2,0,1:T(8,128)S(1)} %maximum_multiply_fusion.1) | copy-start | bytes 1572868
  16.2 22.6 %copy-start.15 = (f32[4608]{0:T(1024)S(1)}, f32[4608]{0:T(1024)}, u32[]{:S(2)}) copy-start(f32[4608]{0:T(1024)} %param.8) | copy-start | bytes 55300
  16.2 95.9 %collective-permute-start.8 = (bf16[512,256]{0,1:T(8,128)(2,1)}, bf16[512,256]{0,1:T(8,128)(2,1)}, u32[]{:S(2)}, u32[]{:S(2)}) collective-permute-start(bf16[512,256]{0,1:T(8,128)(2,1)} %fusion.15), channel_id=1, source_target_pairs={{0,32},{4,36},{8,40},{12,44},{16,48},{20,52},{24,56},{28,60},{32,6... | collective-permute-start | bytes 786440 | tf_op jit(solution)/shard_map/ppermute | solution.py:16
  19.9 96.8 %collective-permute-start.9 = (bf16[512,256]{0,1:T(8,128)(2,1)}, bf16[512,256]{0,1:T(8,128)(2,1)}, u32[]{:S(2)}, u32[]{:S(2)}) collective-permute-start(bf16[512,256]{0,1:T(8,128)(2,1)} %fusion.15), channel_id=1, source_target_pairs={{0,28},{4,32},{8,36},{12,40},{16,44},{20,48},{24,52},{28,56},{32,6... | collective-permute-start | bytes 786440 | tf_op jit(solution)/shard_map/ppermute | solution.py:16
  25.0 93.6 %collective-permute-start.10 = (bf16[512,256]{0,1:T(8,128)(2,1)}, bf16[512,256]{0,1:T(8,128)(2,1)}, u32[]{:S(2)}, u32[]{:S(2)}) collective-permute-start(bf16[512,256]{0,1:T(8,128)(2,1)} %fusion.15), channel_id=1, source_target_pairs={{0,24},{4,28},{8,32},{12,36},{16,40},{20,44},{24,48},{28,52},{32,5... | collective-permute-start | bytes 786440 | tf_op jit(solution)/shard_map/ppermute | solution.py:16
  28.0 92.5 %collective-permute-start.11 = (bf16[512,256]{0,1:T(8,128)(2,1)}, bf16[512,256]{0,1:T(8,128)(2,1)}, u32[]{:S(2)}, u32[]{:S(2)}) collective-permute-start(bf16[512,256]{0,1:T(8,128)(2,1)} %fusion.15), channel_id=1, source_target_pairs={{0,20},{4,24},{8,28},{12,32},{16,36},{20,40},{24,44},{28,48},{32,5... | collective-permute-start | bytes 786440 | tf_op jit(solution)/shard_map/ppermute | solution.py:16
  35.8 94.9 %collective-permute-start = (bf16[512,256]{1,0:T(8,128)(2,1)}, bf16[512,256]{1,0:T(8,128)(2,1)}, u32[]{:S(2)}, u32[]{:S(2)}) collective-permute-start(bf16[512,256]{1,0:T(8,128)(2,1)} %convolution_convert_fusion), channel_id=1, source_target_pairs={{0,32},{4,36},{8,40},{12,44},{16,48},{20,52},{24,56},{28,60},{32,6... | collective-permute-start | bytes 786440 | tf_op jit(solution)/shard_map/ppermute | solution.py:16
  51.4 79.3 %copy-start.8 = (bf16[512,2,2,128]{3,0,2,1:T(8,128)(2,1)}, bf16[512,2,2,128]{3,0,2,1:T(8,128)(2,1)S(1)}, u32[]{:S(2)}) copy-start(bf16[512,2,2,128]{3,0,2,1:T(8,128)(2,1)S(1)} %fusion.14) | copy-start | bytes 1572868
  112.2 25.0 %collective-permute-start.1 = (bf16[512,256]{1,0:T(8,128)(2,1)}, bf16[512,256]{1,0:T(8,128)(2,1)S(1)}, u32[]{:S(2)}, u32[]{:S(2)}) collective-permute-start(bf16[512,256]{1,0:T(8,128)(2,1)} %convolution_convert_fusion), channel_id=1, source_target_pairs={{0,28},{4,32},{8,36},{12,40},{16,44},{20,48},{24,52},{28,56},{32,6... | collective-permute-start | bytes 786440 | tf_op jit(solution)/shard_map/ppermute | solution.py:16
  116.6 26.9 %collective-permute-start.12 = (bf16[512,256]{0,1:T(8,128)(2,1)}, bf16[512,256]{0,1:T(8,128)(2,1)S(1)}, u32[]{:S(2)}, u32[]{:S(2)}) collective-permute-start(bf16[512,256]{0,1:T(8,128)(2,1)} %fusion.15), channel_id=1, source_target_pairs={{0,16},{4,20},{8,24},{12,28},{16,32},{20,36},{24,40},{28,44},{32,4... | collective-permute-start | bytes 786440 | tf_op jit(solution)/shard_map/ppermute | solution.py:16
  118.6 26.9 %collective-permute-start.13 = (bf16[512,256]{0,1:T(8,128)(2,1)}, bf16[512,256]{0,1:T(8,128)(2,1)S(1)}, u32[]{:S(2)}, u32[]{:S(2)}) collective-permute-start(bf16[512,256]{0,1:T(8,128)(2,1)} %fusion.15), channel_id=1, source_target_pairs={{0,12},{4,16},{8,20},{12,24},{16,28},{20,32},{24,36},{28,40},{32,4... | collective-permute-start | bytes 786440 | tf_op jit(solution)/shard_map/ppermute | solution.py:16
  120.5 26.9 %collective-permute-start.2 = (bf16[512,256]{1,0:T(8,128)(2,1)}, bf16[512,256]{1,0:T(8,128)(2,1)S(1)}, u32[]{:S(2)}, u32[]{:S(2)}) collective-permute-start(bf16[512,256]{1,0:T(8,128)(2,1)} %convolution_convert_fusion), channel_id=1, source_target_pairs={{0,24},{4,28},{8,32},{12,36},{16,40},{20,44},{24,48},{28,52},{32,5... | collective-permute-start | bytes 786440 | tf_op jit(solution)/shard_map/ppermute | solution.py:16
  130.7 18.8 %collective-permute-start.3 = (bf16[512,256]{1,0:T(8,128)(2,1)}, bf16[512,256]{1,0:T(8,128)(2,1)S(1)}, u32[]{:S(2)}, u32[]{:S(2)}) collective-permute-start(bf16[512,256]{1,0:T(8,128)(2,1)} %convolution_convert_fusion), channel_id=1, source_target_pairs={{0,20},{4,24},{8,28},{12,32},{16,36},{20,40},{24,44},{28,48},{32,5... | collective-permute-start | bytes 786440 | tf_op jit(solution)/shard_map/ppermute | solution.py:16
  137.1 15.3 %collective-permute-start.4 = (bf16[512,256]{1,0:T(8,128)(2,1)}, bf16[512,256]{1,0:T(8,128)(2,1)S(1)}, u32[]{:S(2)}, u32[]{:S(2)}) collective-permute-start(bf16[512,256]{1,0:T(8,128)(2,1)} %convolution_convert_fusion), channel_id=1, source_target_pairs={{0,16},{4,20},{8,24},{12,28},{16,32},{20,36},{24,40},{28,44},{32,4... | collective-permute-start | bytes 786440 | tf_op jit(solution)/shard_map/ppermute | solution.py:16
  143.5 17.5 %collective-permute-start.14 = (bf16[512,256]{0,1:T(8,128)(2,1)}, bf16[512,256]{0,1:T(8,128)(2,1)}, u32[]{:S(2)}, u32[]{:S(2)}) collective-permute-start(bf16[512,256]{0,1:T(8,128)(2,1)} %fusion.15), channel_id=1, source_target_pairs={{0,8},{4,12},{8,16},{12,20},{16,24},{20,28},{24,32},{28,36},{32,40... | collective-permute-start | bytes 786440 | tf_op jit(solution)/shard_map/ppermute | solution.py:16
  145.4 21.0 %collective-permute-start.15 = (bf16[512,256]{0,1:T(8,128)(2,1)}, bf16[512,256]{0,1:T(8,128)(2,1)}, u32[]{:S(2)}, u32[]{:S(2)}) collective-permute-start(bf16[512,256]{0,1:T(8,128)(2,1)} %fusion.15), channel_id=1, source_target_pairs={{0,4},{4,8},{8,12},{12,16},{16,20},{20,24},{24,28},{28,32},{32,36}... | collective-permute-start | bytes 786440 | tf_op jit(solution)/shard_map/ppermute | solution.py:16
  147.4 20.9 %collective-permute-start.5 = (bf16[512,256]{1,0:T(8,128)(2,1)}, bf16[512,256]{1,0:T(8,128)(2,1)}, u32[]{:S(2)}, u32[]{:S(2)}) collective-permute-start(bf16[512,256]{1,0:T(8,128)(2,1)} %convolution_convert_fusion), channel_id=1, source_target_pairs={{0,12},{4,16},{8,20},{12,24},{16,28},{20,32},{24,36},{28,40},{32,4... | collective-permute-start | bytes 786440 | tf_op jit(solution)/shard_map/ppermute | solution.py:16
  149.6 22.8 %collective-permute-start.6 = (bf16[512,256]{1,0:T(8,128)(2,1)}, bf16[512,256]{1,0:T(8,128)(2,1)}, u32[]{:S(2)}, u32[]{:S(2)}) collective-permute-start(bf16[512,256]{1,0:T(8,128)(2,1)} %convolution_convert_fusion), channel_id=1, source_target_pairs={{0,8},{4,12},{8,16},{12,20},{16,24},{20,28},{24,32},{28,36},{32,40... | collective-permute-start | bytes 786440 | tf_op jit(solution)/shard_map/ppermute | solution.py:16
  152.4 25.4 %collective-permute-start.7 = (bf16[512,256]{1,0:T(8,128)(2,1)}, bf16[512,256]{1,0:T(8,128)(2,1)}, u32[]{:S(2)}, u32[]{:S(2)}) collective-permute-start(bf16[512,256]{1,0:T(8,128)(2,1)} %convolution_convert_fusion), channel_id=1, source_target_pairs={{0,4},{4,8},{8,12},{12,16},{16,20},{20,24},{24,28},{28,32},{32,36}... | collective-permute-start | bytes 786440 | tf_op jit(solution)/shard_map/ppermute | solution.py:16
  182.3 9.8 %copy-start.9 = (bf16[512,2,2,128]{3,0,2,1:T(8,128)(2,1)S(1)}, bf16[512,2,2,128]{3,0,2,1:T(8,128)(2,1)}, u32[]{:S(2)}) copy-start(bf16[512,2,2,128]{3,0,2,1:T(8,128)(2,1)} %copy-done.8) | copy-start | bytes 1572868
  245.1 94.8 %copy-start.12 = (f32[1152]{0:T(1024)S(1)}, f32[1152]{0:T(1024)}, u32[]{:S(2)}) copy-start(f32[1152]{0:T(1024)} %param.13) | copy-start | bytes 13828
  (9 other events, 47.7 us)
Sparse Core Ops, SparseCore 0:
  238.0 90.8 reduce-scatter.1
where the time goes:
time: 352 us; the launch traced here: 351 us
  waiting for transfers between devices  95.5 us (27%)
  blocking collectives  63.2 us (18%)
  matrix products  60 us (17%)
  starting transfers between devices  54.5 us (15%)
  local copies, waits for them, and re-layouts  34.1 us (10%)
  other arithmetic  28.8 us (8%)
  between operations  14.6 us (4%)
    reduce_scatter x1, waiting for transfers between devices, on_device(): lax.psum_scatter(partial_rows, 'tp', scatter_dimension=1, tiled=True)  83.7 us
    psum x1, blocking collectives, spread(): return lax.psum(kept, axis)  54.7 us
    ppermute x16, starting transfers between devices, shifted(): return lax.ppermute(x, axis, pairs)  54.4 us
    dot_general x1, matrix products, one_block(): jnp.einsum('kgql,lkd->qkgd', weight.astype(jnp.bfloat16), value_block, pr...  19.5 us
    dot_general x1, matrix products, one_block(): jnp.einsum('qkgd,lkd->kgql', query, key_block, preferred_element_type=jnp...  17.2 us
    unnamed x52, local copies, waits for them, and re-layouts  14.8 us
    concatenate x10, local copies, waits for them, and re-layouts, on_device(): keys_all = jnp.concatenate([piece[0] for piece in pieces] + [keys], axis=0)  12.6 us
    ppermute x16, waiting for transfers between devices, shifted(): return lax.ppermute(x, axis, pairs)  11.7 us
  transfers between devices with their start and end apart: 17, of which 5 were waited for; matrix products, arithmetic and copies ran while one was open for 14% of the time, Pallas kernels for 0%

commit v1 on v0

v1 whole, which is shorter than its diff:
```python
import jax
import jax.numpy as jnp
from jax import lax
from jax.sharding import PartitionSpec as P

D = 4608
QHEADS = 16
HEAD = 128
WINDOW = 4096
SINKS = 4


def shifted(x, axis, by):
    devices = lax.axis_size(axis)
    pairs = [(i, i + by) for i in range(devices) if 0 <= i + by < devices]
    return lax.ppermute(x, axis, pairs)


def cyclic(x, axis, by):
    devices = lax.axis_size(axis)
    return lax.ppermute(x, axis, [(i, (i + by) % devices) for i in range(devices)])


def rope_tables(positions):
    index = jnp.arange(0, HEAD, 2).astype(jnp.float32)
    inverse = jnp.exp(-jnp.log(jnp.float32(10000.0)) * index / HEAD)
    angles = positions.astype(jnp.float32)[:, None] * inverse[None, :]
    angles = jnp.concatenate([angles, angles], axis=1)
    return (jnp.cos(angles)[:, None, :], jnp.sin(angles)[:, None, :])


def rotate(values, cosine_table, sine_table):
    half = values.shape[-1] // 2
    turned = jnp.concatenate([-values[..., half:], values[..., :half]], axis=-1)
    return values * cosine_table + turned * sine_table


def on_device(hidden_in, pre_gain, w_query, w_key, w_value, w_out, post_gain):
    tok_rows = hidden_in.shape[0]
    local_q = w_query.shape[1] // HEAD
    local_kv = w_key.shape[1] // HEAD
    group = local_q // local_kv
    kv_cols = local_kv * HEAD
    tp_n = lax.axis_size("tp")
    tp_i = lax.axis_index("tp")
    cols_dev = post_gain.shape[0]

    w_blocks = w_out.reshape(w_out.shape[0], tp_n, cols_dev)
    w_recv = []
    for k in range(tp_n):
        part = lax.dynamic_index_in_dim(w_blocks, (tp_i + k) % tp_n, axis=1, keepdims=False)
        w_recv.append(part if k == 0 else cyclic(part, "tp", k))

    offset = lax.axis_index("ctx") * tok_rows
    inputs = hidden_in.astype(jnp.float32)
    normed = (
        inputs * lax.rsqrt(jnp.mean(inputs * inputs, axis=-1, keepdims=True) + 1e-06) * pre_gain
    ).astype(jnp.bfloat16)
    positions = offset + jnp.arange(tok_rows, dtype=jnp.int32)
    cosine_table, sine_table = rope_tables(positions)
    query = jnp.dot(normed, w_query, preferred_element_type=jnp.float32).reshape(
        tok_rows, local_q, HEAD
    )
    query = (
        rotate(query, cosine_table, sine_table)
        .astype(jnp.bfloat16)
        .reshape(tok_rows, local_kv, group, HEAD)
    )
    keys = jnp.dot(normed, w_key, preferred_element_type=jnp.float32).reshape(tok_rows, -1, HEAD)
    keys = rotate(keys, cosine_table, sine_table).astype(jnp.bfloat16).reshape(tok_rows, -1)
    values = jnp.dot(normed, w_value, preferred_element_type=jnp.float32).astype(jnp.bfloat16)
    kv = jnp.concatenate([keys, values], axis=1)

    sink_kv = lax.all_gather(kv[:SINKS], "ctx")[0]
    reach = WINDOW // tok_rows
    pieces = [shifted(kv, "ctx", distance) for distance in range(reach, 0, -1)]
    kv_all = jnp.concatenate(pieces + [kv], axis=0)
    span = WINDOW + tok_rows
    key_block = kv_all[:, :kv_cols].reshape(span, local_kv, HEAD)
    value_block = kv_all[:, kv_cols:].reshape(span, local_kv, HEAD)
    sink_keys = sink_kv[:, :kv_cols].reshape(SINKS, local_kv, HEAD)
    sink_values = sink_kv[:, kv_cols:].reshape(SINKS, local_kv, HEAD)

    scores = (
        jnp.einsum("qkgd,lkd->kgql", query, key_block, preferred_element_type=jnp.float32) / 12.0
    )
    scores = 50.0 * jnp.tanh(scores / 50.0)
    sink_scores = (
        jnp.einsum("qkgd,lkd->kgql", query, sink_keys, preferred_element_type=jnp.float32) / 12.0
    )
    sink_scores = 50.0 * jnp.tanh(sink_scores / 50.0)
    query_pos = positions
    key_pos = offset - WINDOW + jnp.arange(span, dtype=jnp.int32)
    distance_map = query_pos[:, None] - key_pos[None, :]
    live = (key_pos[None, :] >= SINKS) & (distance_map >= 0) & (distance_map < WINDOW)
    sink_live = query_pos[:, None] - jnp.arange(SINKS, dtype=jnp.int32)[None, :] >= 0
    expo = jnp.where(live, jnp.exp(scores), 0.0)
    sink_expo = jnp.where(sink_live, jnp.exp(sink_scores), 0.0)
    sink_sum = jnp.sum(sink_expo, axis=-1)
    total = jnp.sum(expo, axis=-1) + sink_sum
    weight = expo / total[..., None]
    sink_weight = sink_expo / total[..., None]
    attended = jnp.einsum(
        "kgql,lkd->qkgd", weight.astype(jnp.bfloat16), value_block,
        preferred_element_type=jnp.float32,
    )
    attended = attended + jnp.einsum(
        "kgql,lkd->qkgd", sink_weight.astype(jnp.bfloat16), sink_values,
        preferred_element_type=jnp.float32,
    )
    attended = attended.astype(jnp.bfloat16).reshape(tok_rows, local_q * HEAD)
    sink_sums = jnp.sum(sink_sum, axis=(0, 1))

    projected = jnp.dot(attended, w_recv[0], preferred_element_type=jnp.float32)
    for k in range(1, tp_n):
        projected = projected + jnp.dot(
            cyclic(attended, "tp", k), w_recv[k], preferred_element_type=jnp.float32
        )
    squares = jnp.sum(projected * projected, axis=-1)
    total_squares, total_sinks = lax.psum((squares, sink_sums), "tp")
    post = projected * lax.rsqrt(total_squares / D + 1e-06)[:, None] * post_gain
    own_cols = lax.dynamic_slice_in_dim(inputs, tp_i * cols_dev, cols_dev, 1)
    layer_out = (own_cols + post).astype(jnp.bfloat16)
    sink_share = jnp.log(total_sinks / QHEADS)
    return (layer_out, sink_share)


def solution(mesh):
    return jax.shard_map(
        on_device,
        mesh=mesh,
        in_specs=(
            P("ctx", None),
            P(),
            P(None, "tp"),
            P(None, "tp"),
            P(None, "tp"),
            P("tp", None),
            P("tp"),
        ),
        out_specs=(P("ctx", "tp"), P("ctx")),
        check_vma=False,
    )
```

time: 352 us -> 254 us (0.72)
  waiting for transfers between devices: 95.5 us -> 52 us
  starting transfers between devices: 54.5 us -> 33.1 us
  blocking collectives: 63.2 us -> 48.8 us
  between operations: 14.6 us -> 1.17 us
  local copies, waits for them, and re-layouts: 34.1 us -> 25.8 us
  matrix products: 60 us -> 66.3 us
    reduce_scatter x1 -> x0, waiting for transfers between devices: 83.7 us -> none  [on_device(): lax.psum_scatter(partial_rows, 'tp', scatter_dimension=1, tiled=True)]
    psum x1 -> x0, blocking collectives: 54.7 us -> none  [spread(): return lax.psum(kept, axis)]
    all_gather x0 -> x1, blocking collectives: none -> 37.5 us  [on_device(): sink_kv = lax.all_gather(kv[:SINKS], 'ctx')[0]]
    ppermute x0 -> x6, waiting for transfers between devices: none -> 32.1 us  [cyclic(): lax.ppermute(x, axis, [(i, (i + by) % devices) for i in range(devices)])]
    ppermute x16 -> x8, starting transfers between devices: 54.4 us -> 25.7 us  [shifted(): return lax.ppermute(x, axis, pairs)]
    concatenate x11 -> x0, local copies, waits for them, and re-layouts: 13.5 us -> none  [the longest x10 12.6 us: on_device(): keys_all = jnp.concatenate([piece[0] for piece in pieces] + [keys], axis=0)]
    ppermute x16 -> x8, waiting for transfers between devices: 11.7 us -> 19.9 us  [shifted(): return lax.ppermute(x, axis, pairs)]
    ppermute x0 -> x6, starting transfers between devices: none -> 7.36 us  [cyclic(): lax.ppermute(x, axis, [(i, (i + by) % devices) for i in range(devices)])]
  transfers between devices with their start and end apart: 17 -> 14, of which waited for: 5 -> 6; matrix products, arithmetic and copies ran while one was open for 14% -> 38% of each run, Pallas kernels for 0% -> 0%
where the time goes in v1:
time: 254 us; the launch traced here: 253 us
  matrix products  66.3 us (26%)
  waiting for transfers between devices  52 us (20%)
  blocking collectives  48.8 us (19%)
  starting transfers between devices  33.1 us (13%)
  other arithmetic  26.1 us (10%)
  local copies, waits for them, and re-layouts  25.8 us (10%)
    all_gather x1, blocking collectives, on_device(): sink_kv = lax.all_gather(kv[:SINKS], 'ctx')[0]  37.5 us
    ppermute x6, waiting for transfers between devices, cyclic(): lax.ppermute(x, axis, [(i, (i + by) % devices) for i in range(devices)])  32.1 us
    ppermute x8, starting transfers between devices, shifted(): return lax.ppermute(x, axis, pairs)  25.7 us
    dot_general x1, matrix products, on_device(): jnp.einsum('kgql,lkd->qkgd', weight.astype(jnp.bfloat16), value_block, pr...  20.2 us
    ppermute x8, waiting for transfers between devices, shifted(): return lax.ppermute(x, axis, pairs)  19.9 us
    dot_general x1, matrix products, on_device(): jnp.einsum('qkgd,lkd->kgql', query, key_block, preferred_element_type=jnp...  18 us
    unnamed x47, local copies, waits for them, and re-layouts  15.4 us
    psum x1, blocking collectives, on_device(): total_squares, total_sinks = lax.psum((squares, sink_sums), 'tp')  11.4 us
  transfers between devices with their start and end apart: 14, of which 6 were waited for; matrix products, arithmetic and copies ran while one was open for 38% of the time, Pallas kernels for 0%

profile of v1, /device:TPU:8, one launch (start us, length us, event | category | flops | bytes accessed | tf_op | source)
XLA Modules:
  0.0 253.3 jit_solution(4661928804801015121)
XLA Ops:
  0.7 3.5 %multiply_reduce_fusion = f32[512]{0:T(512)S(1)} fusion(bf16[512,4608]{1,0:T(8,128)(2,1)} %param.7), kind=kLoop, calls=%fused_computation.7 | loop fusion | flops 7077376 | bytes 4720640 | tf_op jit(solution)/shard_map/reduce_sum | solution.py:57
  5.5 4.3 %fusion.30 = f32[512,256]{0,1:T(8,128)S(1)} fusion(bf16[4608,256]{1,0:T(8,128)(2,1)S(1)} %copy-done, f32[4608]{0:T(1024)S(1)} %copy-done.17, f32[512]{0:T(512)S(1)} %add_rsqrt_fusion.1, bf16[512,4608]{1,0:T(8,128)(2,1)} %param.7), kind=kOutput, calls=%fused_computation.76 | convolution fusion | flops 1217396736 | bytes 7622656 | tf_op jit(solution)/shard_map/dot_general | solution.py:69
  10.1 4.8 %convolution_convert_fusion = bf16[512,256]{0,1:T(8,128)(2,1)S(1)} fusion(bf16[4608,256]{1,0:T(8,128)(2,1)} %param.11, f32[4608]{0:T(1024)S(1)} %copy-done.17, f32[512]{0:T(512)S(1)} %add_rsqrt_fusion.1, bf16[512,4608]{1,0:T(8,128)(2,1)} %param.7), kind=kOutput, calls=%fused_computation.17 | convolution fusion | flops 1217527808 | bytes 7360512 | tf_op jit(solution)/shard_map/dot_general | solution.py:71
  16.0 3.5 %collective-permute-start = (bf16[512,512]{0,1:T(8,128)(2,1)}, bf16[512,512]{0,1:T(8,128)(2,1)}, u32[]{:S(2)}, u32[]{:S(2)}) collective-permute-start(bf16[512,512]{0,1:T(8,128)(2,1)} %pad_maximum_fusion), channel_id=1, source_target_pairs={{0,32},{4,36},{8,40},{12,44},{16,48},{20,52},{24,56},{28,60},{32,6... | collective-permute-start | bytes 1572872 | tf_op jit(solution)/shard_map/ppermute | solution.py:16
  19.5 5.1 %collective-permute-start.1 = (bf16[512,512]{0,1:T(8,128)(2,1)}, bf16[512,512]{0,1:T(8,128)(2,1)}, u32[]{:S(2)}, u32[]{:S(2)}) collective-permute-start(bf16[512,512]{0,1:T(8,128)(2,1)} %pad_maximum_fusion), channel_id=1, source_target_pairs={{0,28},{4,32},{8,36},{12,40},{16,44},{20,48},{24,52},{28,56},{32,6... | collective-permute-start | bytes 1572872 | tf_op jit(solution)/shard_map/ppermute | solution.py:16
  24.6 3.0 %collective-permute-start.2 = (bf16[512,512]{0,1:T(8,128)(2,1)}, bf16[512,512]{0,1:T(8,128)(2,1)}, u32[]{:S(2)}, u32[]{:S(2)}) collective-permute-start(bf16[512,512]{0,1:T(8,128)(2,1)} %pad_maximum_fusion), channel_id=1, source_target_pairs={{0,24},{4,28},{8,32},{12,36},{16,40},{20,44},{24,48},{28,52},{32,5... | collective-permute-start | bytes 1572872 | tf_op jit(solution)/shard_map/ppermute | solution.py:16
  30.1 4.2 %collective-permute-start.4 = (bf16[512,512]{0,1:T(8,128)(2,1)}, bf16[512,512]{0,1:T(8,128)(2,1)}, u32[]{:S(2)}, u32[]{:S(2)}) collective-permute-start(bf16[512,512]{0,1:T(8,128)(2,1)} %pad_maximum_fusion), channel_id=1, source_target_pairs={{0,16},{4,20},{8,24},{12,28},{16,32},{20,36},{24,40},{28,44},{32,4... | collective-permute-start | bytes 1572872 | tf_op jit(solution)/shard_map/ppermute | solution.py:16
  34.4 6.9 %fusion.29 = f32[512,512]{0,1:T(8,128)S(1)} fusion(bf16[4608,512]{1,0:T(8,128)(2,1)} %param.9, f32[4608]{0:T(1024)S(1)} %copy-done.17, f32[512]{0:T(512)S(1)} %add_rsqrt_fusion.1, bf16[512,4608]{1,0:T(8,128)(2,1)} %param.7), kind=kOutput, calls=%fused_computation.75 | convolution fusion | flops 2425356288 | bytes 10506240 | tf_op jit(solution)/shard_map/dot_general | solution.py:61
  45.3 6.8 %copy.45 = bf16[512,4608]{0,1:T(8,128)(2,1)} copy(bf16[512,4608]{1,0:T(8,128)(2,1)} %param.12) | data formatting | bytes 9437184 | tf_op args[5]
  54.3 4.7 %fusion.3 = pred[512,4608]{0,1:T(8,128)(4,1)} fusion(s32[4608]{0:T(1024)S(1)} %iota_add_fusion, s32[512]{0:T(512)S(1)} %iota_add_fusion.1, pred[4608]{0:T(1024)(128)(4,1)S(1)} %broadcast_compare_fusion), kind=kLoop, calls=%fused_computation.9 | loop fusion | flops 11796480 | bytes 2384384 | tf_op jit(solution)/shard_map/and | solution.py:95
  61.1 37.5 %all-gather.1 = bf16[32,4,512]{2,1,0:T(4,128)(2,1)} all-gather(bf16[1,4,512]{2,1,0:T(4,128)(2,1)S(1)} %copy.43), channel_id=2, replica_groups=mesh['ctx'=32,'tp'=4] {'ctx'}, dimensions={0}, use_global_device_ids=true | all-gather | bytes 135168 | tf_op jit(solution)/shard_map/all_gather | solution.py:74
  108.0 3.3 %collective-permute-start.6 = (bf16[512,512]{0,1:T(8,128)(2,1)}, bf16[512,512]{0,1:T(8,128)(2,1)S(1)}, u32[]{:S(2)}, u32[]{:S(2)}) collective-permute-start(bf16[512,512]{0,1:T(8,128)(2,1)} %pad_maximum_fusion), channel_id=1, source_target_pairs={{0,8},{4,12},{8,16},{12,20},{16,24},{20,28},{24,32},{28,36},{32,40... | collective-permute-start | bytes 1572872 | tf_op jit(solution)/shard_map/ppermute | solution.py:16
  115.6 2.8 %collective-permute-start.13 = (bf16[512,1152]{1,0:T(8,128)(2,1)}, bf16[512,1152]{1,0:T(8,128)(2,1)}, u32[]{:S(2)}, u32[]{:S(2)}) collective-permute-start(bf16[512,1152]{1,0:T(8,128)(2,1)} %bitcast.28), channel_id=1, source_target_pairs={{0,3},{1,0},{2,1},{3,2},{4,7},{5,4},{6,5},{7,6},{8,11},{9,8},{10,9... | collective-permute-start | bytes 3538952 | tf_op jit(solution)/shard_map/ppermute | solution.py:21
  122.1 15.6 %collective-permute-done.6 = bf16[512,512]{0,1:T(8,128)(2,1)S(1)} collective-permute-done((bf16[512,512]{0,1:T(8,128)(2,1)}, bf16[512,512]{0,1:T(8,128)(2,1)S(1)}, u32[]{:S(2)}, u32[]{:S(2)}) %collective-permute-start.6) | collective-permute-done | bytes 524320 | tf_op jit(solution)/shard_map/ppermute | solution.py:16
  137.8 2.9 %collective-permute-done.7 = bf16[512,512]{0,1:T(8,128)(2,1)S(1)} collective-permute-done((bf16[512,512]{0,1:T(8,128)(2,1)}, bf16[512,512]{0,1:T(8,128)(2,1)S(1)}, u32[]{:S(2)}, u32[]{:S(2)}) %collective-permute-start.7) | collective-permute-done | bytes 524320 | tf_op jit(solution)/shard_map/ppermute | solution.py:16
  140.8 2.5 fusion.32
  143.9 18.0 %fusion = (f32[2,2,512]{2,1,0:T(2,128)S(1)}, f32[2,4608,512,2]{2,1,3,0:T(8,128)}) fusion(pred[512,4608]{0,1:T(8,128)(4,1)S(1)} %copy-done.10, bf16[4608,2,128,1]{0,2,3,1:T(8,128)(2,1)} %bitcast.88, bf16[512,2,2,128]{3,0,2,1:T(8,128)(2,1)S(1)} %copy-done.14), kind=kOutput, calls=%fused_computation.2 | convolution fusion | flops 2453665792 | bytes 42999808 | tf_op jit(solution)/shard_map/qkgd,lkd->kgql/dot_general | solution.py:85
  163.0 20.2 %fusion.6 = bf16[2,128,2,512]{3,1,2,0:T(8,128)(2,1)} fusion(f32[2,128,2,512]{3,1,2,0:T(8,128)S(1)} %fusion.22, bf16[4608,2,128,1]{0,2,3,1:T(8,128)(2,1)} %bitcast.87, f32[2,4608,512,2]{2,1,3,0:T(8,128)} %get-tuple-element.18, f32[2,2,512]{2,1,0:T(2,128)S(1)} %add.124, pred[512,4608]{0,1:T(8,128)(4,1)} %fusion.3), kind=kOutput, calls=%fused_computation.16 | convolution fusion | flops 2463629312 | bytes 44048384 | tf_op jit(solution)/shard_map/kgql,lkd->qkgd/dot_general | solution.py:103
  183.1 2.8 %collective-permute-start.12 = (bf16[512,512]{0,1:T(8,128)(2,1)}, bf16[512,512]{0,1:T(8,128)(2,1)}, u32[]{:S(2)}, u32[]{:S(2)}) collective-permute-start(bf16[512,512]{0,1:T(8,128)(2,1)} %bitcast.22), channel_id=1, source_target_pairs={{0,3},{1,0},{2,1},{3,2},{4,7},{5,4},{6,5},{7,6},{8,11},{9,8},{10,9... | collective-permute-start | bytes 1572872 | tf_op jit(solution)/shard_map/ppermute | solution.py:21
  188.1 7.3 %convert_element_type.46 = f32[512,4608]{1,0:T(8,128)} convert(bf16[512,4608]{1,0:T(8,128)(2,1)} %param.7) | non-fusion elementwise | flops 2359296 | bytes 14155776 | tf_op jit(solution)/shard_map/convert_element_type | solution.py:55
  198.6 25.7 %collective-permute-done.12 = bf16[512,512]{0,1:T(8,128)(2,1)} collective-permute-done((bf16[512,512]{0,1:T(8,128)(2,1)}, bf16[512,512]{0,1:T(8,128)(2,1)}, u32[]{:S(2)}, u32[]{:S(2)}) %collective-permute-start.12) | collective-permute-done | bytes 524320 | tf_op jit(solution)/shard_map/ppermute | solution.py:21
  231.3 4.0 %collective-permute-done.10 = bf16[512,512]{0,1:T(8,128)(2,1)S(1)} collective-permute-done((bf16[512,512]{0,1:T(8,128)(2,1)}, bf16[512,512]{0,1:T(8,128)(2,1)S(1)}, u32[]{:S(2)}, u32[]{:S(2)}) %collective-permute-start.10) | collective-permute-done | bytes 524320 | tf_op jit(solution)/shard_map/ppermute | solution.py:21
  237.6 11.4 %all-reduce = (f32[512]{0:T(512)S(1)}, f32[512]{0:T(512)S(1)}) all-reduce(f32[512]{0:T(512)S(1)} %get-tuple-element.20, f32[512]{0:T(512)S(1)} %get-tuple-element.2), channel_id=1, replica_groups=mesh['ctx'=32,'tp'=4] {'tp'}, use_global_device_ids=true, to_apply=%region_4.5 | all-reduce | flops 1024 | bytes 8192 | tf_op jit(solution)/shard_map/psum | solution.py:120
  249.6 3.7 %add_convert_fusion = bf16[512,1152]{1,0:T(8,128)(2,1)} fusion(f32[512,1152]{1,0:T(8,128)} %get-tuple-element.21, f32[512,4608]{1,0:T(8,128)} %convert_element_type.46, s32[]{:T(128)S(6)} %select_n.43, f32[1152]{0:T(1024)S(1)} %copy-done.16, f32[512]{0:T(512)S(1)} %get-tuple-element.23), kind=kLoop, calls=%fused_computation.13 | loop fusion | flops 2359296 | bytes 5904900 | tf_op jit(solution)/shard_map/convert_element_type | solution.py:123
  (97 shorter events, 47.8 us)
Async XLA Ops:
  14.9 19.5 %copy-start.11 = (bf16[512,256]{0,1:T(8,128)(2,1)}, bf16[512,256]{0,1:T(8,128)(2,1)S(1)}, u32[]{:S(2)}) copy-start(bf16[512,256]{0,1:T(8,128)(2,1)S(1)} %convolution_convert_fusion) | copy-start | bytes 786436
  15.1 19.3 %copy-start.4 = (bf16[512,256]{0,1:T(8,128)(2,1)}, bf16[512,256]{0,1:T(8,128)(2,1)S(1)}, u32[]{:S(2)}) copy-start(bf16[512,256]{0,1:T(8,128)(2,1)S(1)} %fusion.17) | copy-start | bytes 786436
  16.0 88.9 %collective-permute-start = (bf16[512,512]{0,1:T(8,128)(2,1)}, bf16[512,512]{0,1:T(8,128)(2,1)}, u32[]{:S(2)}, u32[]{:S(2)}) collective-permute-start(bf16[512,512]{0,1:T(8,128)(2,1)} %pad_maximum_fusion), channel_id=1, source_target_pairs={{0,32},{4,36},{8,40},{12,44},{16,48},{20,52},{24,56},{28,60},{32,6... | collective-permute-start | bytes 1572872 | tf_op jit(solution)/shard_map/ppermute | solution.py:16
  19.5 88.5 %collective-permute-start.1 = (bf16[512,512]{0,1:T(8,128)(2,1)}, bf16[512,512]{0,1:T(8,128)(2,1)}, u32[]{:S(2)}, u32[]{:S(2)}) collective-permute-start(bf16[512,512]{0,1:T(8,128)(2,1)} %pad_maximum_fusion), channel_id=1, source_target_pairs={{0,28},{4,32},{8,36},{12,40},{16,44},{20,48},{24,52},{28,56},{32,6... | collective-permute-start | bytes 1572872 | tf_op jit(solution)/shard_map/ppermute | solution.py:16
  24.6 87.8 %collective-permute-start.2 = (bf16[512,512]{0,1:T(8,128)(2,1)}, bf16[512,512]{0,1:T(8,128)(2,1)}, u32[]{:S(2)}, u32[]{:S(2)}) collective-permute-start(bf16[512,512]{0,1:T(8,128)(2,1)} %pad_maximum_fusion), channel_id=1, source_target_pairs={{0,24},{4,28},{8,32},{12,36},{16,40},{20,44},{24,48},{28,52},{32,5... | collective-permute-start | bytes 1572872 | tf_op jit(solution)/shard_map/ppermute | solution.py:16
  27.6 88.0 %collective-permute-start.3 = (bf16[512,512]{0,1:T(8,128)(2,1)}, bf16[512,512]{0,1:T(8,128)(2,1)}, u32[]{:S(2)}, u32[]{:S(2)}) collective-permute-start(bf16[512,512]{0,1:T(8,128)(2,1)} %pad_maximum_fusion), channel_id=1, source_target_pairs={{0,20},{4,24},{8,28},{12,32},{16,36},{20,40},{24,44},{28,48},{32,5... | collective-permute-start | bytes 1572872 | tf_op jit(solution)/shard_map/ppermute | solution.py:16
  30.1 89.4 %collective-permute-start.4 = (bf16[512,512]{0,1:T(8,128)(2,1)}, bf16[512,512]{0,1:T(8,128)(2,1)}, u32[]{:S(2)}, u32[]{:S(2)}) collective-permute-start(bf16[512,512]{0,1:T(8,128)(2,1)} %pad_maximum_fusion), channel_id=1, source_target_pairs={{0,16},{4,20},{8,24},{12,28},{16,32},{20,36},{24,40},{28,44},{32,4... | collective-permute-start | bytes 1572872 | tf_op jit(solution)/shard_map/ppermute | solution.py:16
  45.3 6.8 %copy-start.3 = (f32[512,2,2,128]{3,0,2,1:T(8,128)S(1)}, f32[512,2,2,128]{3,0,2,1:T(8,128)}, u32[]{:S(2)}) copy-start(f32[512,2,2,128]{3,0,2,1:T(8,128)} %copy.39) | copy-start | bytes 3145732
  45.3 6.8 %copy-start.8 = (f32[512,128]{1,0:T(8,128)S(1)}, f32[512,128]{1,0:T(8,128)}, u32[]{:S(2)}) copy-start(f32[512,128]{1,0:T(8,128)} %copy-done.7) | copy-start | bytes 786436
  52.0 7.0 %copy-start.2 = (bf16[512,4608]{0,1:T(8,128)(2,1)S(1)}, bf16[512,4608]{0,1:T(8,128)(2,1)}, u32[]{:S(2)}) copy-start(bf16[512,4608]{0,1:T(8,128)(2,1)} %copy.45) | copy-start | bytes 14155780
  104.9 35.9 %copy-start.6 = (bf16[512,256]{0,1:T(8,128)(2,1)S(1)}, bf16[512,256]{0,1:T(8,128)(2,1)}, u32[]{:S(2)}) copy-start(bf16[512,256]{0,1:T(8,128)(2,1)} %copy-done.4) | copy-start | bytes 786436
  104.9 35.9 %copy-start.13 = (bf16[512,256]{0,1:T(8,128)(2,1)S(1)}, bf16[512,256]{0,1:T(8,128)(2,1)}, u32[]{:S(2)}) copy-start(bf16[512,256]{0,1:T(8,128)(2,1)} %copy-done.11) | copy-start | bytes 786436
  104.9 17.2 %collective-permute-start.5 = (bf16[512,512]{0,1:T(8,128)(2,1)}, bf16[512,512]{0,1:T(8,128)(2,1)S(1)}, u32[]{:S(2)}, u32[]{:S(2)}) collective-permute-start(bf16[512,512]{0,1:T(8,128)(2,1)} %pad_maximum_fusion), channel_id=1, source_target_pairs={{0,12},{4,16},{8,20},{12,24},{16,28},{20,32},{24,36},{28,40},{32,4... | collective-permute-start | bytes 1572872 | tf_op jit(solution)/shard_map/ppermute | solution.py:16
  108.0 29.7 %collective-permute-start.6 = (bf16[512,512]{0,1:T(8,128)(2,1)}, bf16[512,512]{0,1:T(8,128)(2,1)S(1)}, u32[]{:S(2)}, u32[]{:S(2)}) collective-permute-start(bf16[512,512]{0,1:T(8,128)(2,1)} %pad_maximum_fusion), channel_id=1, source_target_pairs={{0,8},{4,12},{8,16},{12,20},{16,24},{20,28},{24,32},{28,36},{32,40... | collective-permute-start | bytes 1572872 | tf_op jit(solution)/shard_map/ppermute | solution.py:16
  112.4 28.3 %collective-permute-start.7 = (bf16[512,512]{0,1:T(8,128)(2,1)}, bf16[512,512]{0,1:T(8,128)(2,1)S(1)}, u32[]{:S(2)}, u32[]{:S(2)}) collective-permute-start(bf16[512,512]{0,1:T(8,128)(2,1)} %pad_maximum_fusion), channel_id=1, source_target_pairs={{0,4},{4,8},{8,12},{12,16},{16,20},{20,24},{24,28},{28,32},{32,36}... | collective-permute-start | bytes 1572872 | tf_op jit(solution)/shard_map/ppermute | solution.py:16
  115.6 108.7 %collective-permute-start.13 = (bf16[512,1152]{1,0:T(8,128)(2,1)}, bf16[512,1152]{1,0:T(8,128)(2,1)}, u32[]{:S(2)}, u32[]{:S(2)}) collective-permute-start(bf16[512,1152]{1,0:T(8,128)(2,1)} %bitcast.28), channel_id=1, source_target_pairs={{0,3},{1,0},{2,1},{3,2},{4,7},{5,4},{6,5},{7,6},{8,11},{9,8},{10,9... | collective-permute-start | bytes 3538952 | tf_op jit(solution)/shard_map/ppermute | solution.py:21
  119.5 109.5 %collective-permute-start.9 = (bf16[512,1152]{1,0:T(8,128)(2,1)}, bf16[512,1152]{1,0:T(8,128)(2,1)}, u32[]{:S(2)}, u32[]{:S(2)}) collective-permute-start(bf16[512,1152]{1,0:T(8,128)(2,1)} %bitcast.26), channel_id=1, source_target_pairs={{0,1},{1,2},{2,3},{3,0},{4,5},{5,6},{6,7},{7,4},{8,9},{9,10},{10,1... | collective-permute-start | bytes 3538952 | tf_op jit(solution)/shard_map/ppermute | solution.py:21
  143.9 18.1 %copy-start.15 = (f32[2,2,512,4]{2,3,1,0:T(4,128)S(1)}, f32[2,2,512,4]{2,3,1,0:T(4,128)}, u32[]{:S(2)}) copy-start(f32[2,2,512,4]{2,3,1,0:T(4,128)} %get-tuple-element.19) | copy-start | bytes 98308
  183.1 41.2 %collective-permute-start.12 = (bf16[512,512]{0,1:T(8,128)(2,1)}, bf16[512,512]{0,1:T(8,128)(2,1)}, u32[]{:S(2)}, u32[]{:S(2)}) collective-permute-start(bf16[512,512]{0,1:T(8,128)(2,1)} %bitcast.22), channel_id=1, source_target_pairs={{0,3},{1,0},{2,1},{3,2},{4,7},{5,4},{6,5},{7,6},{8,11},{9,8},{10,9... | collective-permute-start | bytes 1572872 | tf_op jit(solution)/shard_map/ppermute | solution.py:21
  187.3 47.9 %collective-permute-start.11 = (bf16[512,1152]{1,0:T(8,128)(2,1)}, bf16[512,1152]{1,0:T(8,128)(2,1)S(1)}, u32[]{:S(2)}, u32[]{:S(2)}) collective-permute-start(bf16[512,1152]{1,0:T(8,128)(2,1)} %bitcast.27), channel_id=1, source_target_pairs={{0,2},{1,3},{2,0},{3,1},{4,6},{5,7},{6,4},{7,5},{8,10},{9,11},{10,... | collective-permute-start | bytes 3538952 | tf_op jit(solution)/shard_map/ppermute | solution.py:21
  195.4 33.7 %collective-permute-start.8 = (bf16[512,512]{0,1:T(8,128)(2,1)}, bf16[512,512]{0,1:T(8,128)(2,1)S(1)}, u32[]{:S(2)}, u32[]{:S(2)}) collective-permute-start(bf16[512,512]{0,1:T(8,128)(2,1)} %bitcast.22), channel_id=1, source_target_pairs={{0,1},{1,2},{2,3},{3,0},{4,5},{5,6},{6,7},{7,4},{8,9},{9,10},{10,1... | collective-permute-start | bytes 1572872 | tf_op jit(solution)/shard_map/ppermute | solution.py:21
  224.3 10.9 %collective-permute-start.10 = (bf16[512,512]{0,1:T(8,128)(2,1)}, bf16[512,512]{0,1:T(8,128)(2,1)S(1)}, u32[]{:S(2)}, u32[]{:S(2)}) collective-permute-start(bf16[512,512]{0,1:T(8,128)(2,1)} %bitcast.22), channel_id=1, source_target_pairs={{0,2},{1,3},{2,0},{3,1},{4,6},{5,7},{6,4},{7,5},{8,10},{9,11},{10,... | collective-permute-start | bytes 1572872 | tf_op jit(solution)/shard_map/ppermute | solution.py:21
  231.2 18.4 %copy-start.16 = (f32[1152]{0:T(1024)S(1)}, f32[1152]{0:T(1024)}, u32[]{:S(2)}) copy-start(f32[1152]{0:T(1024)} %param.13) | copy-start | bytes 13828
  235.2 18.1 %copy-start.1 = (bf16[4608,256]{1,0:T(8,128)(2,1)S(1)}, bf16[4608,256]{1,0:T(8,128)(2,1)}, u32[]{:S(2)}) copy-start(bf16[4608,256]{1,0:T(8,128)(2,1)} %param.10) | copy-start | bytes 7077892
  (8 other events, 34.3 us)

commit v2 on v1

--- a/solution.py
+++ b/solution.py
@@ -1,6 +1,8 @@
 import jax
 import jax.numpy as jnp
 from jax import lax
+from jax.experimental import pallas as pl
+from jax.experimental.pallas import tpu as pltpu
 from jax.sharding import PartitionSpec as P
 
 D = 4608
@@ -33,6 +35,106 @@
     half = values.shape[-1] // 2
     turned = jnp.concatenate([-values[..., half:], values[..., :half]], axis=-1)
     return values * cosine_table + turned * sine_table
+
+
+def window_attention(query2d, kv_all, sink_kv, offset, local_kv, group, tq=256, chunk=256):
+    tok_rows = query2d.shape[0]
+    span = kv_all.shape[0]
+    rows = group * tq
+    win = WINDOW + tq
+    nchunks = win // chunk
+    n_qt = tok_rows // tq
+
+    def kernel(off_ref, q_ref, k_ref, v_ref, sk_ref, sv_ref, o_ref, ss_ref, expo_scr, acc_scr, rs_scr):
+        i = pl.program_id(1)
+        q0 = i * tq
+        base = off_ref[0] - WINDOW + q0
+        qb = q_ref[...]
+        q = jnp.concatenate([qb[:, g * HEAD:(g + 1) * HEAD] for g in range(group)], axis=0)
+        qi = lax.broadcasted_iota(jnp.int32, (rows, 1), 0) % tq
+        lo = jnp.maximum(qi + 1, SINKS - base)
+        hi = qi + WINDOW
+        rs_scr[...] = jnp.zeros((rows, 128), jnp.float32)
+
+        def pass1(c, carry):
+            start = pl.multiple_of(q0 + c * chunk, chunk)
+            kc = k_ref[pl.ds(start, chunk), :]
+            s = lax.dot_general(q, kc, (((1,), (1,)), ((), ())), preferred_element_type=jnp.float32)
+            t = 50.0 * jnp.tanh(s * (1.0 / 600.0))
+            col = c * chunk + lax.broadcasted_iota(jnp.int32, (1, chunk), 1)
+            live = (col >= lo) & (col <= hi)
+            e = jnp.where(live, jnp.exp(t), 0.0)
+            expo_scr[c] = e
+            part = e[:, 0:128]
+            for h in range(1, chunk // 128):
+                part = part + e[:, h * 128:(h + 1) * 128]
+            rs_scr[...] += part
+            return carry
+
+        lax.fori_loop(0, nchunks, pass1, 0)
+        rowsum = jnp.sum(rs_scr[...], axis=1, keepdims=True)
+        qf = q.astype(jnp.float32)
+        skf = sk_ref[...].astype(jnp.float32)
+        qpos = off_ref[0] + q0 + qi
+        sink_e = []
+        for j in range(SINKS):
+            sj = jnp.sum(qf * skf[j:j + 1, :], axis=1, keepdims=True)
+            tj = 50.0 * jnp.tanh(sj * (1.0 / 600.0))
+            sink_e.append(jnp.where(qpos >= j, jnp.exp(tj), 0.0))
+        ssum = sink_e[0]
+        for j in range(1, SINKS):
+            ssum = ssum + sink_e[j]
+        total = rowsum + ssum
+        inv = 1.0 / total
+        acc_scr[...] = jnp.zeros((rows, HEAD), jnp.float32)
+
+        def pass2(c, carry):
+            start = pl.multiple_of(q0 + c * chunk, chunk)
+            w = (expo_scr[c] * inv).astype(jnp.bfloat16)
+            vc = v_ref[pl.ds(start, chunk), :]
+            acc_scr[...] += jnp.dot(w, vc, preferred_element_type=jnp.float32)
+            return carry
+
+        lax.fori_loop(0, nchunks, pass2, 0)
+        out = acc_scr[...]
+        svf = sv_ref[...].astype(jnp.float32)
+        for j in range(SINKS):
+            wj = (sink_e[j] * inv).astype(jnp.bfloat16).astype(jnp.float32)
+            out = out + wj * svf[j:j + 1, :]
+        out16 = out.astype(jnp.bfloat16)
+        for g in range(group):
+            o_ref[:, g * HEAD:(g + 1) * HEAD] = out16[g * tq:(g + 1) * tq]
+            ss_ref[0, g] = ssum[g * tq:(g + 1) * tq]
+
+    off = jnp.reshape(offset, (1,)).astype(jnp.int32)
+    return pl.pallas_call(
+        kernel,
+        out_shape=(
+            jax.ShapeDtypeStruct((tok_rows, local_kv * group * HEAD), jnp.bfloat16),
+            jax.ShapeDtypeStruct((local_kv, group, tok_rows, 1), jnp.float32),
+        ),
+        grid_spec=pltpu.PrefetchScalarGridSpec(
+            num_scalar_prefetch=1,
+            grid=(local_kv, n_qt),
+            in_specs=[
+                pl.BlockSpec((tq, group * HEAD), lambda k, i, o: (i, k)),
+                pl.BlockSpec((span, HEAD), lambda k, i, o: (0, k)),
+                pl.BlockSpec((span, HEAD), lambda k, i, o: (0, local_kv + k)),
+                pl.BlockSpec((SINKS, HEAD), lambda k, i, o: (0, k)),
+                pl.BlockSpec((SINKS, HEAD), lambda k, i, o: (0, local_kv + k)),
+            ],
+            out_specs=[
+                pl.BlockSpec((tq, group * HEAD), lambda k, i, o: (i, k)),
+                pl.BlockSpec((1, group, tq, 1), lambda k, i, o: (k, 0, i, 0)),
+            ],
+            scratch_shapes=[
+                pltpu.VMEM((nchunks, rows, chunk), jnp.float32),
+                pltpu.VMEM((rows, HEAD), jnp.float32),
+                pltpu.VMEM((rows, 128), jnp.float32),
+            ],
+        ),
+        compiler_params=pltpu.CompilerParams(dimension_semantics=("arbitrary", "arbitrary")),
+    )(off, query2d, kv_all, kv_all, sink_kv, sink_kv)
 
 
 def on_device(hidden_in, pre_gain, w_query, w_key, w_value, w_out, post_gain):
@@ -75,41 +177,8 @@
     reach = WINDOW // tok_rows
     pieces = [shifted(kv, "ctx", distance) for distance in range(reach, 0, -1)]
     kv_all = jnp.concatenate(pieces + [kv], axis=0)
-    span = WINDOW + tok_rows
-    key_block = kv_all[:, :kv_cols].reshape(span, local_kv, HEAD)
-    value_block = kv_all[:, kv_cols:].reshape(span, local_kv, HEAD)
-    sink_keys = sink_kv[:, :kv_cols].reshape(SINKS, local_kv, HEAD)
-    sink_values = sink_kv[:, kv_cols:].reshape(SINKS, local_kv, HEAD)
-
-    scores = (
-        jnp.einsum("qkgd,lkd->kgql", query, key_block, preferred_element_type=jnp.float32) / 12.0
-    )
-    scores = 50.0 * jnp.tanh(scores / 50.0)
-    sink_scores = (
-        jnp.einsum("qkgd,lkd->kgql", query, sink_keys, preferred_element_type=jnp.float32) / 12.0
-    )
-    sink_scores = 50.0 * jnp.tanh(sink_scores / 50.0)
-    query_pos = positions
-    key_pos = offset - WINDOW + jnp.arange(span, dtype=jnp.int32)
-    distance_map = query_pos[:, None] - key_pos[None, :]
-    live = (key_pos[None, :] >= SINKS) & (distance_map >= 0) & (distance_map < WINDOW)
-    sink_live = query_pos[:, None] - jnp.arange(SINKS, dtype=jnp.int32)[None, :] >= 0
-    expo = jnp.where(live, jnp.exp(scores), 0.0)
-    sink_expo = jnp.where(sink_live, jnp.exp(sink_scores), 0.0)
-    sink_sum = jnp.sum(sink_expo, axis=-1)
-    total = jnp.sum(expo, axis=-1) + sink_sum
-    weight = expo / total[..., None]
-    sink_weight = sink_expo / total[..., None]
-    attended = jnp.einsum(
-        "kgql,lkd->qkgd", weight.astype(jnp.bfloat16), value_block,
-        preferred_element_type=jnp.float32,
-    )
-    attended = attended + jnp.einsum(
-        "kgql,lkd->qkgd", sink_weight.astype(jnp.bfloat16), sink_values,
-        preferred_element_type=jnp.float32,
-    )
-    attended = attended.astype(jnp.bfloat16).reshape(tok_rows, local_q * HEAD)
-    sink_sums = jnp.sum(sink_sum, axis=(0, 1))
+    attended, sink_parts = window_attention(query.reshape(tok_rows, -1), kv_all, sink_kv, offset, local_kv, group)
+    sink_sums = jnp.sum(sink_parts[..., 0], axis=(0, 1))
 
     projected = jnp.dot(attended, w_recv[0], preferred_element_type=jnp.float32)
     for k in range(1, tp_n):

time: 254 us -> 254 us (level)
  Pallas kernels: 0 us -> 45.7 us
  matrix products: 66.3 us -> 23.2 us
  waiting for transfers between devices: 52 us -> 39 us
  local copies, waits for them, and re-layouts: 25.8 us -> 30.8 us
  blocking collectives: 48.8 us -> 53.2 us
  starting transfers between devices: 33.1 us -> 36.8 us
  other arithmetic: 26.1 us -> 23.4 us
    pallas_call x0 -> x1, Pallas kernels: none -> 45.7 us  [window_attention(): pl.pallas_call(kernel, out_shape=(jax.ShapeDtypeStruct((tok_rows, local_k...]
    dot_general x4 -> x0, matrix products: 41.2 us -> none  [the longest x1 20.2 us: on_device(): jnp.einsum('kgql,lkd->qkgd', weight.astype(jnp.bfloat16), value_block, pr...]
    ppermute x6, waiting for transfers between devices: 32.1 us -> 24.9 us  [cyclic(): lax.ppermute(x, axis, [(i, (i + by) % devices) for i in range(devices)])]
    ppermute x8, waiting for transfers between devices: 19.9 us -> 14.1 us  [shifted(): return lax.ppermute(x, axis, pairs)]
    unnamed x47 -> x43, local copies, waits for them, and re-layouts: 15.4 us -> 20.7 us
    and x1 -> x0, other arithmetic: 4.75 us -> none  [on_device(): (key_pos[None, :] >= SINKS) & (distance_map >= 0) & (distance_map < WINDOW)]
    ppermute x6, starting transfers between devices: 7.36 us -> 11.1 us  [cyclic(): lax.ppermute(x, axis, [(i, (i + by) % devices) for i in range(devices)])]
    psum x1, blocking collectives: 11.4 us -> 14.4 us  [on_device(): total_squares, total_sinks = lax.psum((squares, sink_sums), 'tp')]
  transfers between devices with their start and end apart: 14 -> 14, of which waited for: 6 -> 4; matrix products, arithmetic and copies ran while one was open for 38% -> 22% of each run, Pallas kernels for 0% -> 18%
where the time goes in v2:
time: 254 us; the launch traced here: 253 us
  blocking collectives  53.2 us (21%)
  Pallas kernels  45.7 us (18%)
  waiting for transfers between devices  39 us (15%)
  starting transfers between devices  36.8 us (14%)
  local copies, waits for them, and re-layouts  30.8 us (12%)
  other arithmetic  23.4 us (9%)
  matrix products  23.2 us (9%)
    pallas_call x1, Pallas kernels, window_attention(): pl.pallas_call(kernel, out_shape=(jax.ShapeDtypeStruct((tok_rows, local_k...  45.7 us
    all_gather x1, blocking collectives, on_device(): sink_kv = lax.all_gather(kv[:SINKS], 'ctx')[0]  38.7 us
    ppermute x8, starting transfers between devices, shifted(): return lax.ppermute(x, axis, pairs)  25.7 us
    ppermute x6, waiting for transfers between devices, cyclic(): lax.ppermute(x, axis, [(i, (i + by) % devices) for i in range(devices)])  24.9 us
    unnamed x43, local copies, waits for them, and re-layouts  20.7 us
    psum x1, blocking collectives, on_device(): total_squares, total_sinks = lax.psum((squares, sink_sums), 'tp')  14.4 us
    ppermute x8, waiting for transfers between devices, shifted(): return lax.ppermute(x, axis, pairs)  14.1 us
    ppermute x6, starting transfers between devices, cyclic(): lax.ppermute(x, axis, [(i, (i + by) % devices) for i in range(devices)])  11.1 us
  transfers between devices with their start and end apart: 14, of which 4 were waited for; matrix products, arithmetic and copies ran while one was open for 22% of the time, Pallas kernels for 18%

profile of v2, /device:TPU:8, one launch (start us, length us, event | category | flops | bytes accessed | tf_op | source)
XLA Modules:
  0.0 253.2 jit_solution(1933411690358005606)
XLA Ops:
  0.7 3.5 %multiply_reduce_fusion = f32[512]{0:T(512)S(1)} fusion(bf16[512,4608]{1,0:T(8,128)(2,1)} %param.7), kind=kLoop, calls=%fused_computation.1 | loop fusion | flops 7077376 | bytes 4720640 | tf_op jit(solution)/shard_map/reduce_sum | solution.py:159
  5.1 2.5 fusion.10
  9.9 4.6 %convolution_convert_fusion = bf16[512,256]{1,0:T(8,128)(2,1)S(1)} fusion(bf16[4608,256]{1,0:T(8,128)(2,1)} %param.11, f32[4608]{0:T(1024)S(1)} %copy-done.14, f32[512]{0:T(512)S(1)} %add_rsqrt_fusion.1, bf16[512,4608]{1,0:T(8,128)(2,1)} %param.7), kind=kOutput, calls=%fused_computation.7 | convolution fusion | flops 1217527808 | bytes 7360512 | tf_op jit(solution)/shard_map/dot_general | solution.py:173
  16.4 3.5 %collective-permute-start = (bf16[512,512]{1,0:T(8,128)(2,1)}, bf16[512,512]{1,0:T(8,128)(2,1)}, u32[]{:S(2)}, u32[]{:S(2)}) collective-permute-start(bf16[512,512]{1,0:T(8,128)(2,1)} %pad_maximum_fusion), channel_id=1, source_target_pairs={{0,32},{4,36},{8,40},{12,44},{16,48},{20,52},{24,56},{28,60},{32,6... | collective-permute-start | bytes 1572872 | tf_op jit(solution)/shard_map/ppermute | solution.py:18
  19.9 5.1 %collective-permute-start.1 = (bf16[512,512]{1,0:T(8,128)(2,1)}, bf16[512,512]{1,0:T(8,128)(2,1)}, u32[]{:S(2)}, u32[]{:S(2)}) collective-permute-start(bf16[512,512]{1,0:T(8,128)(2,1)} %pad_maximum_fusion), channel_id=1, source_target_pairs={{0,28},{4,32},{8,36},{12,40},{16,44},{20,48},{24,52},{28,56},{32,6... | collective-permute-start | bytes 1572872 | tf_op jit(solution)/shard_map/ppermute | solution.py:18
  25.0 3.0 %collective-permute-start.2 = (bf16[512,512]{1,0:T(8,128)(2,1)}, bf16[512,512]{1,0:T(8,128)(2,1)}, u32[]{:S(2)}, u32[]{:S(2)}) collective-permute-start(bf16[512,512]{1,0:T(8,128)(2,1)} %pad_maximum_fusion), channel_id=1, source_target_pairs={{0,24},{4,28},{8,32},{12,36},{16,40},{20,44},{24,48},{28,52},{32,5... | collective-permute-start | bytes 1572872 | tf_op jit(solution)/shard_map/ppermute | solution.py:18
  28.0 2.5 collective-permute-start.3
  30.5 4.2 %collective-permute-start.4 = (bf16[512,512]{1,0:T(8,128)(2,1)}, bf16[512,512]{1,0:T(8,128)(2,1)}, u32[]{:S(2)}, u32[]{:S(2)}) collective-permute-start(bf16[512,512]{1,0:T(8,128)(2,1)} %pad_maximum_fusion), channel_id=1, source_target_pairs={{0,16},{4,20},{8,24},{12,28},{16,32},{20,36},{24,40},{28,44},{32,4... | collective-permute-start | bytes 1572872 | tf_op jit(solution)/shard_map/ppermute | solution.py:18
  34.8 6.9 %fusion.11 = f32[512,512]{0,1:T(8,128)S(1)} fusion(bf16[4608,512]{1,0:T(8,128)(2,1)} %param.9, f32[4608]{0:T(1024)S(1)} %copy-done.14, f32[512]{0:T(512)S(1)} %add_rsqrt_fusion.1, bf16[512,4608]{1,0:T(8,128)(2,1)} %param.7), kind=kOutput, calls=%fused_computation.47 | convolution fusion | flops 2425356288 | bytes 10506240 | tf_op jit(solution)/shard_map/dot_general | solution.py:163
  44.1 6.6 %copy.42 = bf16[512,4608]{0,1:T(8,128)(2,1)} copy(bf16[512,4608]{1,0:T(8,128)(2,1)} %param.12) | data formatting | bytes 9437184 | tf_op args[5]
  52.4 2.3 constant_dynamic-slice_fusion.1
  55.9 2.3 fusion.3.q_ref
  58.2 38.7 %all-gather.1 = bf16[32,4,512]{2,1,0:T(4,128)(2,1)S(1)} all-gather(bf16[1,4,512]{2,1,0:T(4,128)(2,1)S(1)} %fusion.8), channel_id=2, replica_groups=mesh['ctx'=32,'tp'=4] {'ctx'}, dimensions={0}, use_global_device_ids=true | all-gather | bytes 135168 | tf_op jit(solution)/shard_map/all_gather | solution.py:176
  104.3 3.3 %collective-permute-start.6 = (bf16[512,512]{1,0:T(8,128)(2,1)}, bf16[512,512]{1,0:T(8,128)(2,1)S(1)}, u32[]{:S(2)}, u32[]{:S(2)}) collective-permute-start(bf16[512,512]{1,0:T(8,128)(2,1)} %pad_maximum_fusion), channel_id=1, source_target_pairs={{0,8},{4,12},{8,16},{12,20},{16,24},{20,28},{24,32},{28,36},{32,40... | collective-permute-start | bytes 1572872 | tf_op jit(solution)/shard_map/ppermute | solution.py:18
  121.2 11.2 %collective-permute-done.6 = bf16[512,512]{1,0:T(8,128)(2,1)S(1)} collective-permute-done((bf16[512,512]{1,0:T(8,128)(2,1)}, bf16[512,512]{1,0:T(8,128)(2,1)S(1)}, u32[]{:S(2)}, u32[]{:S(2)}) %collective-permute-start.6) | collective-permute-done | bytes 524320 | tf_op jit(solution)/shard_map/ppermute | solution.py:18
  133.3 2.9 %collective-permute-done.7 = bf16[512,512]{1,0:T(8,128)(2,1)S(1)} collective-permute-done((bf16[512,512]{1,0:T(8,128)(2,1)}, bf16[512,512]{1,0:T(8,128)(2,1)S(1)}, u32[]{:S(2)}, u32[]{:S(2)}) %collective-permute-start.7) | collective-permute-done | bytes 524320 | tf_op jit(solution)/shard_map/ppermute | solution.py:18
  137.8 45.7 %shard_map.86 = (bf16[512,512]{1,0:T(8,128)(2,1)}, f32[2,2,512,1]{3,2,1,0:T(8,128)}) custom-call(s32[1]{0:T(128)} %bitcast.off_ref, bf16[512,512]{1,0:T(8,128)(2,1)} %fusion.3.q_ref, bf16[4608,512]{1,0:T(8,128)(2,1)} %constant_dynamic-update-slice_fusion.k_ref.v_ref, bf16[4608,512]{1,0:T(8,128)(2,1)} %constant_dynamic-update-slice_fusion.k_ref.v_ref, ...), custom_call_target="tpu_custom_call" | custom-call | tf_op jit(solution)/shard_map/pallas_call | solution.py:110
  190.0 7.3 %convert_element_type.34 = f32[512,4608]{1,0:T(8,128)} convert(bf16[512,4608]{1,0:T(8,128)(2,1)} %param.7) | non-fusion elementwise | flops 2359296 | bytes 14155776 | tf_op jit(solution)/shard_map/convert_element_type | solution.py:157
  198.8 2.8 %collective-permute-start.10 = (bf16[512,512]{1,0:T(8,128)(2,1)}, bf16[512,512]{1,0:T(8,128)(2,1)S(1)}, u32[]{:S(2)}, u32[]{:S(2)}) collective-permute-start(bf16[512,512]{1,0:T(8,128)(2,1)} %get-tuple-element.4), channel_id=1, source_target_pairs={{0,2},{1,3},{2,0},{3,1},{4,6},{5,7},{6,4},{7,5},{8,10},{9,11},{10,... | collective-permute-start | bytes 1572872 | tf_op jit(solution)/shard_map/ppermute | solution.py:23
  206.1 2.3 convolution_add_fusion.1
  208.5 23.6 %collective-permute-done.10 = bf16[512,512]{1,0:T(8,128)(2,1)S(1)} collective-permute-done((bf16[512,512]{1,0:T(8,128)(2,1)}, bf16[512,512]{1,0:T(8,128)(2,1)S(1)}, u32[]{:S(2)}, u32[]{:S(2)}) %collective-permute-start.10) | collective-permute-done | bytes 524320 | tf_op jit(solution)/shard_map/ppermute | solution.py:23
  232.1 2.3 multiply_reduce_fusion.1
  234.4 14.4 %all-reduce = (f32[512]{0:T(512)S(1)}, f32[512]{0:T(512)S(1)}) all-reduce(f32[512]{0:T(512)S(1)} %get-tuple-element.17, f32[512]{0:T(512)S(1)} %reduce_sum.29), channel_id=1, replica_groups=mesh['ctx'=32,'tp'=4] {'tp'}, use_global_device_ids=true, to_apply=%region_2.3 | all-reduce | flops 1024 | bytes 8192 | tf_op jit(solution)/shard_map/psum | solution.py:189
  249.4 3.7 %add_convert_fusion = bf16[512,1152]{1,0:T(8,128)(2,1)} fusion(f32[512,1152]{1,0:T(8,128)} %get-tuple-element.18, f32[512,4608]{1,0:T(8,128)} %convert_element_type.34, s32[]{:T(128)S(6)} %select_n.35, f32[1152]{0:T(1024)S(1)} %copy-done.13, f32[512]{0:T(512)S(1)} %get-tuple-element.20), kind=kLoop, calls=%fused_computation.5 | loop fusion | flops 2359296 | bytes 5904900 | tf_op jit(solution)/shard_map/convert_element_type | solution.py:192
  (87 shorter events, 46.8 us)
Async XLA Ops:
  9.9 5.3 %copy-start.7 = (f32[512,128]{1,0:T(8,128)}, f32[512,128]{1,0:T(8,128)S(1)}, u32[]{:S(2)}) copy-start(f32[512,128]{1,0:T(8,128)S(1)} %get-tuple-element.15) | copy-start | bytes 786436
  14.5 20.2 %copy-start.8 = (bf16[512,256]{1,0:T(8,128)(2,1)}, bf16[512,256]{1,0:T(8,128)(2,1)S(1)}, u32[]{:S(2)}) copy-start(bf16[512,256]{1,0:T(8,128)(2,1)S(1)} %convolution_convert_fusion) | copy-start | bytes 786436
  15.5 19.3 %copy-start.4 = (bf16[512,256]{1,0:T(8,128)(2,1)}, bf16[512,256]{1,0:T(8,128)(2,1)S(1)}, u32[]{:S(2)}) copy-start(bf16[512,256]{1,0:T(8,128)(2,1)S(1)} %fusion.4) | copy-start | bytes 786436
  16.4 84.0 %collective-permute-start = (bf16[512,512]{1,0:T(8,128)(2,1)}, bf16[512,512]{1,0:T(8,128)(2,1)}, u32[]{:S(2)}, u32[]{:S(2)}) collective-permute-start(bf16[512,512]{1,0:T(8,128)(2,1)} %pad_maximum_fusion), channel_id=1, source_target_pairs={{0,32},{4,36},{8,40},{12,44},{16,48},{20,52},{24,56},{28,60},{32,6... | collective-permute-start | bytes 1572872 | tf_op jit(solution)/shard_map/ppermute | solution.py:18
  19.9 84.4 %collective-permute-start.1 = (bf16[512,512]{1,0:T(8,128)(2,1)}, bf16[512,512]{1,0:T(8,128)(2,1)}, u32[]{:S(2)}, u32[]{:S(2)}) collective-permute-start(bf16[512,512]{1,0:T(8,128)(2,1)} %pad_maximum_fusion), channel_id=1, source_target_pairs={{0,28},{4,32},{8,36},{12,40},{16,44},{20,48},{24,52},{28,56},{32,6... | collective-permute-start | bytes 1572872 | tf_op jit(solution)/shard_map/ppermute | solution.py:18
  25.0 84.5 %collective-permute-start.2 = (bf16[512,512]{1,0:T(8,128)(2,1)}, bf16[512,512]{1,0:T(8,128)(2,1)}, u32[]{:S(2)}, u32[]{:S(2)}) collective-permute-start(bf16[512,512]{1,0:T(8,128)(2,1)} %pad_maximum_fusion), channel_id=1, source_target_pairs={{0,24},{4,28},{8,32},{12,36},{16,40},{20,44},{24,48},{28,52},{32,5... | collective-permute-start | bytes 1572872 | tf_op jit(solution)/shard_map/ppermute | solution.py:18
  28.0 85.4 %collective-permute-start.3 = (bf16[512,512]{1,0:T(8,128)(2,1)}, bf16[512,512]{1,0:T(8,128)(2,1)}, u32[]{:S(2)}, u32[]{:S(2)}) collective-permute-start(bf16[512,512]{1,0:T(8,128)(2,1)} %pad_maximum_fusion), channel_id=1, source_target_pairs={{0,20},{4,24},{8,28},{12,32},{16,36},{20,40},{24,44},{28,48},{32,5... | collective-permute-start | bytes 1572872 | tf_op jit(solution)/shard_map/ppermute | solution.py:18
  30.5 86.3 %collective-permute-start.4 = (bf16[512,512]{1,0:T(8,128)(2,1)}, bf16[512,512]{1,0:T(8,128)(2,1)}, u32[]{:S(2)}, u32[]{:S(2)}) collective-permute-start(bf16[512,512]{1,0:T(8,128)(2,1)} %pad_maximum_fusion), channel_id=1, source_target_pairs={{0,16},{4,20},{8,24},{12,28},{16,32},{20,36},{24,40},{28,44},{32,4... | collective-permute-start | bytes 1572872 | tf_op jit(solution)/shard_map/ppermute | solution.py:18
  52.4 5.8 %copy-start.5 = (bf16[512,256]{1,0:T(8,128)(2,1)S(1)}, bf16[512,256]{1,0:T(8,128)(2,1)}, u32[]{:S(2)}) copy-start(bf16[512,256]{1,0:T(8,128)(2,1)} %copy-done.4) | copy-start | bytes 786436
  52.4 5.8 %copy-start.9 = (bf16[512,256]{1,0:T(8,128)(2,1)S(1)}, bf16[512,256]{1,0:T(8,128)(2,1)}, u32[]{:S(2)}) copy-start(bf16[512,256]{1,0:T(8,128)(2,1)} %copy-done.8) | copy-start | bytes 786436
  100.3 36.6 %copy-start.6 = (bf16[512,256]{1,0:T(8,128)(2,1)S(1)}, bf16[512,256]{1,0:T(8,128)(2,1)}, u32[]{:S(2)}) copy-start(bf16[512,256]{1,0:T(8,128)(2,1)} %copy-done.4) | copy-start | bytes 786436
  100.3 36.6 %copy-start.10 = (bf16[512,256]{1,0:T(8,128)(2,1)S(1)}, bf16[512,256]{1,0:T(8,128)(2,1)}, u32[]{:S(2)}) copy-start(bf16[512,256]{1,0:T(8,128)(2,1)} %copy-done.8) | copy-start | bytes 786436
  100.3 20.1 %collective-permute-start.5 = (bf16[512,512]{1,0:T(8,128)(2,1)}, bf16[512,512]{1,0:T(8,128)(2,1)S(1)}, u32[]{:S(2)}, u32[]{:S(2)}) collective-permute-start(bf16[512,512]{1,0:T(8,128)(2,1)} %pad_maximum_fusion), channel_id=1, source_target_pairs={{0,12},{4,16},{8,20},{12,24},{16,28},{20,32},{24,36},{28,40},{32,4... | collective-permute-start | bytes 1572872 | tf_op jit(solution)/shard_map/ppermute | solution.py:18
  104.3 28.2 %collective-permute-start.6 = (bf16[512,512]{1,0:T(8,128)(2,1)}, bf16[512,512]{1,0:T(8,128)(2,1)S(1)}, u32[]{:S(2)}, u32[]{:S(2)}) collective-permute-start(bf16[512,512]{1,0:T(8,128)(2,1)} %pad_maximum_fusion), channel_id=1, source_target_pairs={{0,8},{4,12},{8,16},{12,20},{16,24},{20,28},{24,32},{28,36},{32,40... | collective-permute-start | bytes 1572872 | tf_op jit(solution)/shard_map/ppermute | solution.py:18
  109.4 26.7 %collective-permute-start.7 = (bf16[512,512]{1,0:T(8,128)(2,1)}, bf16[512,512]{1,0:T(8,128)(2,1)S(1)}, u32[]{:S(2)}, u32[]{:S(2)}) collective-permute-start(bf16[512,512]{1,0:T(8,128)(2,1)} %pad_maximum_fusion), channel_id=1, source_target_pairs={{0,4},{4,8},{8,12},{12,16},{16,20},{20,24},{24,28},{28,32},{32,36}... | collective-permute-start | bytes 1572872 | tf_op jit(solution)/shard_map/ppermute | solution.py:18
  113.4 88.1 %collective-permute-start.9 = (bf16[512,1152]{1,0:T(8,128)(2,1)}, bf16[512,1152]{1,0:T(8,128)(2,1)}, u32[]{:S(2)}, u32[]{:S(2)}) collective-permute-start(bf16[512,1152]{1,0:T(8,128)(2,1)} %bitcast.7), channel_id=1, source_target_pairs={{0,1},{1,2},{2,3},{3,0},{4,5},{5,6},{6,7},{7,4},{8,9},{9,10},{10,1... | collective-permute-start | bytes 3538952 | tf_op jit(solution)/shard_map/ppermute | solution.py:23
  116.8 87.1 %collective-permute-start.13 = (bf16[512,1152]{1,0:T(8,128)(2,1)}, bf16[512,1152]{1,0:T(8,128)(2,1)}, u32[]{:S(2)}, u32[]{:S(2)}) collective-permute-start(bf16[512,1152]{1,0:T(8,128)(2,1)} %bitcast.9), channel_id=1, source_target_pairs={{0,3},{1,0},{2,1},{3,2},{4,7},{5,4},{6,5},{7,6},{8,11},{9,8},{10,9... | collective-permute-start | bytes 3538952 | tf_op jit(solution)/shard_map/ppermute | solution.py:23
  183.5 15.2 %collective-permute-start.8 = (bf16[512,512]{1,0:T(8,128)(2,1)}, bf16[512,512]{1,0:T(8,128)(2,1)S(1)}, u32[]{:S(2)}, u32[]{:S(2)}) collective-permute-start(bf16[512,512]{1,0:T(8,128)(2,1)} %get-tuple-element.4), channel_id=1, source_target_pairs={{0,1},{1,2},{2,3},{3,0},{4,5},{5,6},{6,7},{7,4},{8,9},{9,10},{10,1... | collective-permute-start | bytes 1572872 | tf_op jit(solution)/shard_map/ppermute | solution.py:23
  185.0 18.8 %collective-permute-start.12 = (bf16[512,512]{1,0:T(8,128)(2,1)}, bf16[512,512]{1,0:T(8,128)(2,1)}, u32[]{:S(2)}, u32[]{:S(2)}) collective-permute-start(bf16[512,512]{1,0:T(8,128)(2,1)} %get-tuple-element.4), channel_id=1, source_target_pairs={{0,3},{1,0},{2,1},{3,2},{4,7},{5,4},{6,5},{7,6},{8,11},{9,8},{10,9... | collective-permute-start | bytes 1572872 | tf_op jit(solution)/shard_map/ppermute | solution.py:23
  188.2 43.9 %collective-permute-start.11 = (bf16[512,1152]{1,0:T(8,128)(2,1)}, bf16[512,1152]{1,0:T(8,128)(2,1)S(1)}, u32[]{:S(2)}, u32[]{:S(2)}) collective-permute-start(bf16[512,1152]{1,0:T(8,128)(2,1)} %bitcast.8), channel_id=1, source_target_pairs={{0,2},{1,3},{2,0},{3,1},{4,6},{5,7},{6,4},{7,5},{8,10},{9,11},{10,... | collective-permute-start | bytes 3538952 | tf_op jit(solution)/shard_map/ppermute | solution.py:23
  190.0 7.3 %copy-start.12 = (f32[2,2,512,1]{3,2,1,0:T(8,128)S(1)}, f32[2,2,512,1]{3,2,1,0:T(8,128)}, u32[]{:S(2)}) copy-start(f32[2,2,512,1]{3,2,1,0:T(8,128)} %get-tuple-element.5) | copy-start | bytes 24580
  198.8 33.3 %collective-permute-start.10 = (bf16[512,512]{1,0:T(8,128)(2,1)}, bf16[512,512]{1,0:T(8,128)(2,1)S(1)}, u32[]{:S(2)}, u32[]{:S(2)}) collective-permute-start(bf16[512,512]{1,0:T(8,128)(2,1)} %get-tuple-element.4), channel_id=1, source_target_pairs={{0,2},{1,3},{2,0},{3,1},{4,6},{5,7},{6,4},{7,5},{8,10},{9,11},{10,... | collective-permute-start | bytes 1572872 | tf_op jit(solution)/shard_map/ppermute | solution.py:23
  208.5 41.0 %copy-start.13 = (f32[1152]{0:T(1024)S(1)}, f32[1152]{0:T(1024)}, u32[]{:S(2)}) copy-start(f32[1152]{0:T(1024)} %param.13) | copy-start | bytes 13828
  232.1 21.1 %copy-start.1 = (bf16[4608,256]{1,0:T(8,128)(2,1)S(1)}, bf16[4608,256]{1,0:T(8,128)(2,1)}, u32[]{:S(2)}) copy-start(bf16[4608,256]{1,0:T(8,128)(2,1)} %param.10) | copy-start | bytes 7077892
  (5 other events, 16.5 us)
